TPU v7x, 32 devices: a whole 2x2x4 slice. The times are simulated.
32 devices in a mesh: dp: 16 (over z, x, core), mp: 2 (over y).
Axes of the slice: x: 2, y: 2, z: 4, core: 2. Of those that a mesh axis runs over, the one named last changes fastest.
Arguments:
- tokens: bfloat16 [16384, 768], P('dp'), may hold values from -6 to 6
- doc_ids: int32 [16, 1024], P('dp'), may hold values from 0 to 3, never falling along the last dimension, each value on 1 to 512 neighbouring positions
- ln1_gain: bfloat16 [768], replicated, may hold values from 0.25 to 1.75
- ln1_bias: bfloat16 [768], replicated, may hold values from -2.5 to 2.5
- w_qkv: bfloat16 [768, 3, 768], P(None, None, 'mp'), may hold values from -0.21875 to 0.21875
- b_qv: bfloat16 [2, 768], P(None, 'mp'), may hold values from -3 to 3
- w_out: bfloat16 [768, 768], P('mp'), may hold values from -1.75 to 1.75
- b_out: bfloat16 [768], replicated, may hold values from -3 to 3
- ln2_gain: bfloat16 [768], replicated, may hold values from 0.25 to 1.75
- ln2_bias: bfloat16 [768], replicated, may hold values from -2.5 to 2.5
- w_up: bfloat16 [768, 3072], P(None, 'mp'), may hold values from -0.21875 to 0.21875
- b_up: bfloat16 [3072], P('mp'), may hold values from -3 to 3
- w_down: bfloat16 [3072, 768], P('mp'), may hold values from -0.15625 to 0.15625
- b_down: bfloat16 [768], replicated, may hold values from -3 to 3
- cotangent: bfloat16 [16384, 768], P('dp'), may hold values from -6 to 6
Outputs:
- block_out: bfloat16 [16384, 768], P('dp')
- grad_tokens: float32 [16384, 768], P('dp')
- grad_ln1_gain: float32 [768], replicated
- grad_ln1_bias: float32 [768], replicated
- grad_w_qkv: float32 [768, 3, 768], P('dp', None, 'mp')
- grad_b_qv: float32 [2, 768], P(None, 'mp')
- grad_w_out: float32 [768, 768], P('mp', 'dp')
- grad_b_out: float32 [768], replicated
- grad_ln2_gain: float32 [768], replicated
- grad_ln2_bias: float32 [768], replicated
- grad_w_up: float32 [768, 3072], P('dp', 'mp')
- grad_b_up: float32 [3072], P('mp')
- grad_w_down: float32 [3072, 768], P('mp', 'dp')
- grad_b_down: float32 [768], replicated
Inputs may be any that keep to these rules, and one draw needn't show every extreme that they name: `doc_ids`: within each packed row the ids start at 0, never fall, and each id covers 1 to 512 consecutive positions, one of them exactly that many.
All inputs are finite; a program needn't handle non-finite values.
Results may differ from a plain program's by a relative error of at most 0.009.
Values may be sent and summed in bfloat16 or wider, within the bound.
No kernel may reach another device: no remote copies, remote signals or barrier semaphores. Data moves between devices by JAX's collectives and lax.ppermute only.
A program may use at most 192 MiB of HBM per device.

v0:
```python
import math

import jax
import jax.numpy as jnp
from jax import lax
from jax.sharding import PartitionSpec as P

HD = 64


epsilon = 1e-05


def normalize(values):
    average = jnp.mean(values, axis=-1, keepdims=True)
    centered = values - average
    variance = jnp.mean(centered * centered, axis=-1, keepdims=True)
    inverse = lax.rsqrt(variance + epsilon)
    return (centered * inverse, inverse)


def norm_back(grad_out, normal_rows, inverse, gain):
    grad_unit = grad_out * gain
    return inverse * (
        grad_unit
        - jnp.mean(grad_unit, axis=-1, keepdims=True)
        - normal_rows * jnp.mean(grad_unit * normal_rows, axis=-1, keepdims=True)
    )


def gelu_tanh(values):
    return (
        0.5
        * values
        * (1.0 + jnp.tanh(0.7978845608028654 * (values + 0.044715 * values * values * values)))
    )


def block_scores(query_block, key_rows, doc_rows, offset):
    block_rows = query_block.shape[0]
    scores = jnp.einsum(
        "qhd,khd->hqk", query_block, key_rows, preferred_element_type=jnp.float32
    ) * (1.0 / math.sqrt(HD))
    query_pos = offset + lax.iota(jnp.int32, block_rows)
    key_pos = lax.iota(jnp.int32, key_rows.shape[0])
    block_docs = doc_rows[offset : offset + block_rows]
    allowed = (block_docs[:, None] == doc_rows[None, :]) & (query_pos[:, None] >= key_pos[None, :])
    return jnp.where(allowed[None], scores, -1e30)


def attend_forward(queries, key_rows, value_rows, doc_rows):
    seq_len = queries.shape[0]
    block_rows = min(512, seq_len)
    outputs = []
    log_parts = []
    for offset in range(0, seq_len, block_rows):
        scores = block_scores(queries[offset : offset + block_rows], key_rows, doc_rows, offset)
        row_max = jnp.max(scores, axis=-1, keepdims=True)
        log_total = row_max + jnp.log(jnp.sum(jnp.exp(scores - row_max), axis=-1, keepdims=True))
        probabilities = jnp.exp(scores - log_total).astype(jnp.bfloat16)
        outputs.append(
            jnp.einsum(
                "hqk,khd->qhd", probabilities, value_rows, preferred_element_type=jnp.float32
            )
        )
        log_parts.append(log_total[..., 0])
    return (jnp.concatenate(outputs, axis=0), jnp.concatenate(log_parts, axis=1))


def attend_backward(queries, key_rows, value_rows, doc_rows, log_totals, grad_out):
    seq_len = queries.shape[0]
    block_rows = min(512, seq_len)
    scale_factor = 1.0 / math.sqrt(HD)
    grad_queries = []
    grad_keys = jnp.zeros(key_rows.shape, jnp.float32)
    grad_values = jnp.zeros(value_rows.shape, jnp.float32)
    for offset in range(0, seq_len, block_rows):
        query_block = queries[offset : offset + block_rows]
        grad_block = grad_out[offset : offset + block_rows]
        scores = block_scores(query_block, key_rows, doc_rows, offset)
        probabilities = jnp.exp(scores - log_totals[:, offset : offset + block_rows, None])
        grad_probs = jnp.einsum(
            "qhd,khd->hqk", grad_block, value_rows, preferred_element_type=jnp.float32
        )
        row_dots = jnp.sum(probabilities * grad_probs, axis=-1, keepdims=True)
        grad_scores = (probabilities * (grad_probs - row_dots)).astype(jnp.bfloat16)
        grad_queries.append(
            scale_factor
            * jnp.einsum("hqk,khd->qhd", grad_scores, key_rows, preferred_element_type=jnp.float32)
        )
        grad_keys = grad_keys + scale_factor * jnp.einsum(
            "hqk,qhd->khd", grad_scores, query_block, preferred_element_type=jnp.float32
        )
        grad_values = grad_values + jnp.einsum(
            "hqk,qhd->khd",
            probabilities.astype(jnp.bfloat16),
            grad_block,
            preferred_element_type=jnp.float32,
        )
    return (jnp.concatenate(grad_queries, axis=0), grad_keys, grad_values)


def shards(
    tokens,
    doc_ids,
    ln1_gain,
    ln1_bias,
    w_qkv,
    b_qv,
    w_out,
    b_out,
    ln2_gain,
    ln2_bias,
    w_up,
    b_up,
    w_down,
    b_down,
    cotangent,
):
    row_count = tokens.shape[0]
    local_width = w_qkv.shape[2]
    seq_count, seq_len = doc_ids.shape
    seq_shape = (seq_count, seq_len, local_width // HD, HD)
    token_rows = tokens.astype(jnp.float32)
    normal_one, inv_one = normalize(token_rows)
    gain_one = ln1_gain.astype(jnp.float32)
    normed_one = (normal_one * gain_one + ln1_bias.astype(jnp.float32)).astype(jnp.bfloat16)
    projected = jnp.einsum("td,dce->tce", normed_one, w_qkv, preferred_element_type=jnp.float32)
    bias_qv = b_qv.astype(jnp.float32)
    queries = (projected[:, 0] + bias_qv[0]).astype(jnp.bfloat16).reshape(seq_shape)
    key_rows = projected[:, 1].astype(jnp.bfloat16).reshape(seq_shape)
    value_rows = (projected[:, 2] + bias_qv[1]).astype(jnp.bfloat16).reshape(seq_shape)
    attended, log_totals = lax.map(
        lambda packed: attend_forward(*packed), (queries, key_rows, value_rows, doc_ids)
    )
    mixed = attended.reshape(row_count, local_width).astype(jnp.bfloat16)
    attn_part = jnp.dot(mixed, w_out, preferred_element_type=jnp.float32)
    gain_two = ln2_gain.astype(jnp.float32)
    after_attn = token_rows + lax.psum(attn_part, "mp") + b_out.astype(jnp.float32)
    normal_two, inv_two = normalize(after_attn)
    normed_two = (normal_two * gain_two + ln2_bias.astype(jnp.float32)).astype(jnp.bfloat16)
    up_rows = jnp.dot(normed_two, w_up, preferred_element_type=jnp.float32) + b_up.astype(
        jnp.float32
    )
    activated, gelu_pull = jax.vjp(gelu_tanh, up_rows)
    act_rows = activated.astype(jnp.bfloat16)
    ffn_part = jnp.dot(act_rows, w_down, preferred_element_type=jnp.float32)
    bias_down = b_down.astype(jnp.float32)
    cot_rows = cotangent.astype(jnp.float32)
    block_out = (
        after_attn + (lax.psum(ffn_part.astype(jnp.bfloat16), "mp").astype(jnp.float32) + bias_down)
    ).astype(jnp.bfloat16)
    grad_w_down = jnp.einsum("tf,td->fd", act_rows, cotangent, preferred_element_type=jnp.float32)
    grad_act = jnp.einsum("td,fd->tf", cotangent, w_down, preferred_element_type=jnp.float32)
    grad_up = gelu_pull(grad_act)[0].astype(jnp.bfloat16)
    grad_w_up = jnp.einsum("td,tf->df", normed_two, grad_up, preferred_element_type=jnp.float32)
    grad_b_up = jnp.sum(grad_up.astype(jnp.float32), axis=0)
    norm_two_part = jnp.einsum("tf,df->td", grad_up, w_up, preferred_element_type=jnp.float32)
    grad_normed_two = lax.psum(norm_two_part, "mp")
    grad_after = cot_rows + norm_back(grad_normed_two, normal_two, inv_two, gain_two)
    grad_attn_here = grad_after.astype(jnp.bfloat16)
    grad_w_out = jnp.einsum("te,td->ed", mixed, grad_attn_here, preferred_element_type=jnp.float32)
    grad_mixed = jnp.einsum(
        "td,ed->te", grad_attn_here, w_out, preferred_element_type=jnp.float32
    ).astype(jnp.bfloat16)
    grad_q, grad_k, grad_v = lax.map(
        lambda packed: attend_backward(*packed),
        (queries, key_rows, value_rows, doc_ids, log_totals, grad_mixed.reshape(seq_shape)),
    )
    grad_q = grad_q.reshape(row_count, local_width).astype(jnp.bfloat16)
    grad_k = grad_k.reshape(row_count, local_width).astype(jnp.bfloat16)
    grad_v = grad_v.reshape(row_count, local_width).astype(jnp.bfloat16)
    grad_proj = jnp.stack([grad_q, grad_k, grad_v], axis=1)
    grad_w_qkv = jnp.einsum(
        "td,tce->dce", normed_one, grad_proj, preferred_element_type=jnp.float32
    )
    grad_b_qv = jnp.stack(
        [jnp.sum(grad_q.astype(jnp.float32), axis=0), jnp.sum(grad_v.astype(jnp.float32), axis=0)]
    )
    norm_one_part = jnp.einsum("tce,dce->td", grad_proj, w_qkv, preferred_element_type=jnp.float32)
    grad_normed_one = lax.psum(norm_one_part, "mp")
    normal_here, inv_here = (normal_one, inv_one)
    grad_input = grad_after + norm_back(grad_normed_one, normal_here, inv_here, gain_one)
    vector_terms = jnp.stack(
        [
            jnp.sum(grad_normed_one * normal_here, axis=0),
            jnp.sum(grad_normed_one, axis=0),
            jnp.sum(grad_normed_two * normal_two, axis=0),
            jnp.sum(grad_normed_two, axis=0),
            jnp.sum(grad_attn_here.astype(jnp.float32), axis=0),
            jnp.sum(cot_rows, axis=0),
        ]
    )
    vector_sum, qv_sum, up_sum = lax.psum((vector_terms, grad_b_qv, grad_b_up), "dp")
    sum_qkv, sum_out, sum_up, sum_down = (
        lax.psum_scatter(grad_w_qkv, "dp", scatter_dimension=0, tiled=True),
        lax.psum_scatter(grad_w_out, "dp", scatter_dimension=1, tiled=True),
        lax.psum_scatter(grad_w_up, "dp", scatter_dimension=0, tiled=True),
        lax.psum_scatter(grad_w_down, "dp", scatter_dimension=1, tiled=True),
    )
    return (
        block_out,
        grad_input,
        vector_sum[0],
        vector_sum[1],
        sum_qkv,
        qv_sum,
        sum_out,
        vector_sum[4],
        vector_sum[2],
        vector_sum[3],
        sum_up,
        up_sum,
        sum_down,
        vector_sum[5],
    )


def solution(mesh):
    return jax.shard_map(
        shards,
        mesh=mesh,
        in_specs=(
            P("dp", None),
            P("dp", None),
            P(),
            P(),
            P(None, None, "mp"),
            P(None, "mp"),
            P("mp", None),
            P(),
            P(),
            P(),
            P(None, "mp"),
            P("mp"),
            P("mp", None),
            P(),
            P("dp", None),
        ),
        out_specs=(
            P("dp", None),
            P("dp", None),
            P(),
            P(),
            P("dp", None, "mp"),
            P(None, "mp"),
            P("mp", "dp"),
            P(),
            P(),
            P(),
            P("dp", "mp"),
            P("mp"),
            P("mp", "dp"),
            P(),
        ),
        check_vma=False,
    )
```

profile of v0, /device:TPU:0, one launch (start us, length us, event | category | flops | bytes accessed | tf_op | source)
XLA Modules:
  0.0 773.5 jit_solution(16983525216406019219)
XLA Ops:
  35.9 9.0 %fusion.32 = bf16[512,6,64]{0,2,1:T(8,128)(2,1)S(1)} fusion(bf16[1024,6,64]{0,2,1:T(8,128)(2,1)S(1)} %add_convert_fusion.3, f32[6,512,1024]{2,1,0:T(8,128)} %copy-done.3, f32[6,512]{1,0:T(8,128)S(1)} %log_add_fusion.1, pred[512,1024]{1,0:T(8,128)(4,1)S(1)} %get-tuple-element.99), kind=kOutput, calls=%fused_computation.80 | convolution fusion | flops 415432704 | bytes 14299136 | tf_op jit(solution)/shard_map/while/body/eval_jaxpr/hqk,khd->qhd/dot_general | solution.py:62
  57.6 83.5 %all-reduce.6.cloned.1.call-done = f32[1024,768]{1,0:T(8,128)} async-done(((f32[1024,768]{1,0:T(8,128)}), f32[1024,768]{1,0:T(8,128)}) %all-reduce.6.cloned.1.call-update) | async-done | bytes 3145744 | tf_op jit(solution)/shard_map/psum | solution.py:139
  149.7 10.3 %convert_reduce_fusion = (f32[1536]{0:T(1024)}, bf16[1024,1536]{1,0:T(8,128)(2,1)S(1)}, bf16[1024,1536]{1,0:T(8,128)(2,1)}) fusion(f32[1024,1536]{1,0:T(8,128)S(1)} %fusion.49, f32[1536]{0:T(1024)S(1)} %copy-done.53, bf16[1024,768]{1,0:T(8,128)(2,1)S(1)} %copy-done.22, bf16[1536,768]{1,0:T(8,128)(2,1)S(1)} %copy-done), kind=kOutput, calls=%fused_computation.24 | convolution fusion | flops 2461530624 | bytes 16527360 | tf_op jit(solution)/shard_map/td,fd->tf/dot_general | solution.py:154
  166.1 5.6 convolution_convert_fusion
  172.5 79.5 %all-reduce.10.cloned.1.call-done = f32[1024,768]{1,0:T(8,128)} async-done(((f32[1024,768]{1,0:T(8,128)}), f32[1024,768]{1,0:T(8,128)}) %all-reduce.10.cloned.1.call-update) | async-done | bytes 3145744 | tf_op jit(solution)/shard_map/psum | solution.py:159
  256.4 50.1 %all-reduce.8.cloned.1.call-done = bf16[1024,768]{1,0:T(8,128)(2,1)} async-done(((bf16[1024,768]{1,0:T(8,128)(2,1)}), bf16[1024,768]{1,0:T(8,128)(2,1)}) %all-reduce.8.cloned.1.call-update) | async-done | bytes 1572880 | tf_op jit(solution)/shard_map/psum | solution.py:151
  306.5 5.7 convert_reduce_fusion.3
  313.8 6.6 fusion.45
  320.4 10.2 %multiply_reduce_fusion.1 = (f32[6,512]{1,0:T(8,128)S(1)}, f32[6,512,1024]{2,1,0:T(8,128)}) fusion(f32[6,512,1024]{2,1,0:T(8,128)} %copy-done.3, f32[6,512]{1,0:T(8,128)S(1)} %copy-done.31, pred[512,1024]{1,0:T(8,128)(4,1)S(1)} %copy-done.12, bf16[512,6,64]{0,2,1:T(8,128)(2,1)S(1)} %bitcast.92, bf16[1024,6,64]{0,2,1:T(8,128)(2,1)S(1)} %copy-done.14), kind=kOutput, calls=%fused_computation.3 | convolution fusion | flops 418378752 | bytes 26894336 | tf_op jit(solution)/shard_map/while/body/eval_jaxpr/qhd,khd->hqk/dot_general | solution.py:82
  330.7 7.5 multiply_reduce_fusion
  338.1 17.8 %multiply_convert_fusion = (bf16[6,512,1024]{2,1,0:T(8,128)(2,1)}, bf16[6,512,1024]{2,1,0:T(8,128)(2,1)}) fusion(f32[6,512,1024]{2,1,0:T(8,128)} %get-tuple-element.110, f32[6,512,1024]{2,1,0:T(8,128)S(1)} %bitcast.75, f32[6,512]{1,0:T(8,128)S(1)} %get-tuple-element.109, f32[6,512]{1,0:T(8,128)S(1)} %log_add_fusion, pred[512,1024]{1,0:T(8,128)(4,1)S(1)} %copy-done.10, ...), kind=kLoop, calls=%fused_computation | loop fusion | flops 37748736 | bytes 64012288 | tf_op jit(solution)/shard_map/while/body/eval_jaxpr/convert_element_type | solution.py:86
  355.9 5.7 fusion.31
  362.9 5.3 convert_reduce_fusion.4
  370.5 5.6 fusion.30
  382.4 5.7 convolution_bitcast_fusion
  393.3 6.9 fusion.59
  400.9 7.9 %fusion.48 = f32[768,1536]{1,0:T(8,128)} fusion(bf16[1024,1536]{1,0:T(8,128)(2,1)} %copy-done.62, f32[1024,768]{1,0:T(8,128)} %copy-done.6, f32[768]{0:T(1024)S(1)} %copy-done.58, f32[768]{0:T(1024)S(1)} %copy-done.43, f32[1024]{0:T(1024)S(1)} %copy-done.46, f32[1024]{0:T(1024)S(1)} %copy-done.36), kind=kOutput, calls=%fused_computation.111 | convolution fusion | flops 2419851264 | bytes 11024384 | tf_op jit(solution)/shard_map/td,tf->df/dot_general | solution.py:156
  410.7 5.4 fusion.34
  417.0 57.1 %all-reduce.12.cloned.1.call-done = f32[1024,768]{1,0:T(8,128)} async-done(((f32[1024,768]{1,0:T(8,128)}), f32[1024,768]{1,0:T(8,128)}) %all-reduce.12.cloned.1.call-update) | async-done | bytes 3145744 | tf_op jit(solution)/shard_map/psum | solution.py:181
  477.2 61.8 %all-reduce = (f32[6,768]{1,0:T(8,128)S(1)}, f32[2,384]{1,0:T(2,128)}, f32[1536]{0:T(1024)}) all-reduce(f32[6,768]{1,0:T(8,128)S(1)} %stack.43, f32[2,384]{1,0:T(2,128)S(1)} %pad_maximum_fusion.4, f32[1536]{0:T(1024)S(1)} %copy-done.54), channel_id=1, replica_groups=mesh['dp'=16,'mp'=2] {'dp'}, use_global_device_ids=true, to_apply=%region_24.25 | all-reduce | flops 6912 | bytes 55296 | tf_op jit(solution)/shard_map/psum | solution.py:194
  539.7 5.1 fusion.21
  544.8 70.5 %reduce-scatter.11.cloned.1.call-done = f32[1536,48]{0,1:T(8,128)} async-done(((f32[1536,768]{0,1:T(8,128)}), f32[1536,48]{0,1:T(8,128)}) %reduce-scatter.11.cloned.1.call-update) | async-done | bytes 294928 | tf_op jit(solution)/shard_map/reduce_scatter | solution.py:199
  615.3 79.2 %reduce-scatter.9.cloned.1.call-done = f32[48,1536]{1,0:T(8,128)} async-done(((f32[768,1536]{1,0:T(8,128)}), f32[48,1536]{1,0:T(8,128)}) %reduce-scatter.9.cloned.1.call-update) | async-done | bytes 294928 | tf_op jit(solution)/shard_map/reduce_scatter | solution.py:198
  694.5 71.8 %reduce-scatter.5.cloned.1.call-done = f32[48,3,384]{2,0,1:T(8,128)} async-done(((f32[768,3,384]{2,0,1:T(8,128)}), f32[48,3,384]{2,0,1:T(8,128)}) %reduce-scatter.5.cloned.1.call-update) | async-done | bytes 221200 | tf_op jit(solution)/shard_map/reduce_scatter | solution.py:196
  (215 shorter events, 84.5 us)
Async XLA Ops:
  7.2 142.5 %copy-start = (bf16[1536,768]{1,0:T(8,128)(2,1)S(1)}, bf16[1536,768]{1,0:T(8,128)(2,1)}, u32[]{:S(2)}) copy-start(bf16[1536,768]{1,0:T(8,128)(2,1)} %param.27) | copy-start | bytes 7077892
  7.2 134.0 %all-reduce.6.cloned.1.call-start = ((), (), s32[]{:S(2)}) async-start(), calls=%async_computation.4 | async-start | bytes 6291456 | tf_op jit(solution)/shard_map/psum | solution.py:139
  8.1 8.4 %copy-start.37 = (f32[768]{0:T(1024)}, f32[768]{0:T(1024)S(1)}, u32[]{:S(2)}) copy-start(f32[768]{0:T(1024)S(1)} %convert_element_type.157) | copy-start | bytes 9220
  22.6 13.3 %copy-start.11 = (pred[512,1024]{1,0:T(8,128)(4,1)}, pred[512,1024]{1,0:T(8,128)(4,1)S(1)}, u32[]{:S(2)}) copy-start(pred[512,1024]{1,0:T(8,128)(4,1)S(1)} %get-tuple-element.99) | copy-start | bytes 1572868
  22.6 22.3 %copy-start.9 = (pred[512,1024]{1,0:T(8,128)(4,1)}, pred[512,1024]{1,0:T(8,128)(4,1)S(1)}, u32[]{:S(2)}) copy-start(pred[512,1024]{1,0:T(8,128)(4,1)S(1)} %get-tuple-element.100) | copy-start | bytes 1572868
  31.9 12.9 %copy-start.2 = (f32[6,512,1024]{2,1,0:T(8,128)}, f32[6,512,1024]{2,1,0:T(8,128)S(1)}, u32[]{:S(2)}) copy-start(f32[6,512,1024]{2,1,0:T(8,128)S(1)} %get-tuple-element.104) | copy-start | bytes 37748740
  35.8 9.0 %copy-start.13 = (bf16[1024,6,64]{0,2,1:T(8,128)(2,1)}, bf16[1024,6,64]{0,2,1:T(8,128)(2,1)S(1)}, u32[]{:S(2)}) copy-start(bf16[1024,6,64]{0,2,1:T(8,128)(2,1)S(1)} %add_convert_fusion.3) | copy-start | bytes 2359300
  52.5 199.6 %all-reduce.10.cloned.1.call-start = ((), (), s32[]{:S(2)}) async-start(), calls=%async_computation.6 | async-start | bytes 6291456 | tf_op jit(solution)/shard_map/psum | solution.py:159
  166.1 140.4 %all-reduce.8.cloned.1.call-start = ((), (), s32[]{:S(2)}) async-start(), calls=%async_computation.5 | async-start | bytes 3145728 | tf_op jit(solution)/shard_map/psum | solution.py:151
  171.8 302.3 %all-reduce.12.cloned.1.call-start = ((), (), s32[]{:S(2)}) async-start(), calls=%async_computation.7 | async-start | bytes 6291456 | tf_op jit(solution)/shard_map/psum | solution.py:181
  172.5 134.0 %copy-start.23 = (bf16[1024,768]{1,0:T(8,128)(2,1)S(1)}, bf16[1024,768]{1,0:T(8,128)(2,1)}, u32[]{:S(2)}) copy-start(bf16[1024,768]{1,0:T(8,128)(2,1)} %param.29) | copy-start | bytes 4718596
  172.5 134.0 %copy-start.35 = (f32[1024]{0:T(1024)S(1)}, f32[1024]{0:T(1024)}, u32[]{:S(2)}) copy-start(f32[1024]{0:T(1024)} %copy-done.34) | copy-start | bytes 12292
  172.5 134.0 %copy-start.42 = (f32[768]{0:T(1024)S(1)}, f32[768]{0:T(1024)}, u32[]{:S(2)}) copy-start(f32[768]{0:T(1024)} %convert_element_type.168) | copy-start | bytes 9220
  172.5 134.0 %copy-start.45 = (f32[1024]{0:T(1024)S(1)}, f32[1024]{0:T(1024)}, u32[]{:S(2)}) copy-start(f32[1024]{0:T(1024)} %copy-done.44) | copy-start | bytes 12292
  313.8 16.8 %slice-start = ((s8[12582912]{0:T(1024)(128)(4,1)}), s8[4194304]{0:T(1024)(128)(4,1)S(1)}, s32[]{:S(2)}) async-start(s8[12582912]{0:T(1024)(128)(4,1)} %bitcast.74), calls=%async_computation.12 | async-start | bytes 8388608
  313.8 16.8 %slice-start.1 = ((s8[12582912]{0:T(1024)(128)(4,1)}), s8[4194304]{0:T(1024)(128)(4,1)S(1)}, s32[]{:S(2)}) async-start(s8[12582912]{0:T(1024)(128)(4,1)} %bitcast.74), calls=%async_computation.13 | async-start | bytes 8388608
  320.4 10.3 %slice-start.2 = ((s8[12582912]{0:T(1024)(128)(4,1)}), s8[4194304]{0:T(1024)(128)(4,1)S(1)}, s32[]{:S(2)}) async-start(s8[12582912]{0:T(1024)(128)(4,1)} %bitcast.74), calls=%async_computation.14 | async-start | bytes 8388608
  320.4 10.2 %copy-start.10 = (pred[512,1024]{1,0:T(8,128)(4,1)S(1)}, pred[512,1024]{1,0:T(8,128)(4,1)}, u32[]{:S(2)}) copy-start(pred[512,1024]{1,0:T(8,128)(4,1)} %copy-done.9) | copy-start | bytes 1572868
  388.1 156.7 %reduce-scatter.7.cloned.1.call-start = ((), (), s32[]{:S(2)}) async-start(), calls=%async_computation.9 | async-start | bytes 1253376 | tf_op jit(solution)/shard_map/reduce_scatter | solution.py:197
  393.2 222.1 %reduce-scatter.11.cloned.1.call-start = ((), (), s32[]{:S(2)}) async-start(), calls=%async_computation.11 | async-start | bytes 5013504 | tf_op jit(solution)/shard_map/reduce_scatter | solution.py:199
  400.2 294.3 %reduce-scatter.9.cloned.1.call-start = ((), (), s32[]{:S(2)}) async-start(), calls=%async_computation.10 | async-start | bytes 5013504 | tf_op jit(solution)/shard_map/reduce_scatter | solution.py:198
  408.9 357.4 %reduce-scatter.5.cloned.1.call-start = ((), (), s32[]{:S(2)}) async-start(), calls=%async_computation.8 | async-start | bytes 3760128 | tf_op jit(solution)/shard_map/reduce_scatter | solution.py:196
  416.1 61.1 %copy-start.54 = (f32[1536]{0:T(1024)S(1)}, f32[1536]{0:T(1024)}, u32[]{:S(2)}) copy-start(f32[1536]{0:T(1024)} %get-tuple-element.84) | copy-start | bytes 18436
  539.7 226.7 %copy-start.1 = (bf16[1536,768]{1,0:T(8,128)(2,1)S(1)}, bf16[1536,768]{1,0:T(8,128)(2,1)}, u32[]{:S(2)}) copy-start(bf16[1536,768]{1,0:T(8,128)(2,1)} %param.27) | copy-start | bytes 7077892
  (51 other events, 145.4 us)
Sparse Core Ops, SparseCore 0:
  52.6 88.5 all-reduce.5
  166.2 85.8 all-reduce.9
  254.9 51.5 all-reduce.7
  388.2 85.8 all-reduce.11
  478.1 58.1 reduce-scatter.6
  540.6 74.6 reduce-scatter.10
  619.7 74.7 reduce-scatter.8
  698.9 67.3 reduce-scatter.4
where the time goes:
time: 778 us; the launch traced here: 773 us
  waiting for transfers between devices  492 us (63%)
  matrix products  124 us (16%)
  other arithmetic  62.7 us (8%)
  blocking collectives  61.8 us (8%)
  local copies, waits for them, and re-layouts  17.3 us (2%)
  between operations  15.2 us (2%)
    psum x1, waiting for transfers between devices, shards(): lax.psum(attn_part, 'mp')  83.5 us
    psum x1, waiting for transfers between devices, shards(): grad_normed_two = lax.psum(norm_two_part, 'mp')  79.5 us
    reduce_scatter x1, waiting for transfers between devices, shards(): lax.psum_scatter(grad_w_up, 'dp', scatter_dimension=0, tiled=True)  79.2 us
    reduce_scatter x1, waiting for transfers between devices, shards(): lax.psum_scatter(grad_w_qkv, 'dp', scatter_dimension=0, tiled=True)  71.8 us
    reduce_scatter x1, waiting for transfers between devices, shards(): lax.psum_scatter(grad_w_down, 'dp', scatter_dimension=1, tiled=True)  70.5 us
    psum x1, blocking collectives, shards(): lax.psum((vector_terms, grad_b_qv, grad_b_up), 'dp')  61.8 us
    psum x1, waiting for transfers between devices, shards(): grad_normed_one = lax.psum(norm_one_part, 'mp')  57.1 us
    psum x1, waiting for transfers between devices, shards(): lax.psum(ffn_part.astype(jnp.bfloat16), 'mp').astype(jnp.float32)  50.1 us
  transfers between devices with their start and end apart: 8, of which 7 were waited for; matrix products, arithmetic and copies ran while one was open for 6% of the time, Pallas kernels for 0%

commit v1 on v0

v1 whole, which is shorter than its diff:
```python
import math

import jax
import jax.numpy as jnp
from jax import lax
from jax.sharding import PartitionSpec as P

HD = 64


epsilon = 1e-05


def normalize(values):
    average = jnp.mean(values, axis=-1, keepdims=True)
    centered = values - average
    variance = jnp.mean(centered * centered, axis=-1, keepdims=True)
    inverse = lax.rsqrt(variance + epsilon)
    return (centered * inverse, inverse)


def norm_back(grad_out, normal_rows, inverse, gain):
    grad_unit = grad_out * gain
    return inverse * (
        grad_unit
        - jnp.mean(grad_unit, axis=-1, keepdims=True)
        - normal_rows * jnp.mean(grad_unit * normal_rows, axis=-1, keepdims=True)
    )


def gelu_tanh(values):
    return (
        0.5
        * values
        * (1.0 + jnp.tanh(0.7978845608028654 * (values + 0.044715 * values * values * values)))
    )


def block_scores(query_block, key_rows, doc_rows, offset):
    block_rows = query_block.shape[0]
    scores = jnp.einsum(
        "qhd,khd->hqk", query_block, key_rows, preferred_element_type=jnp.float32
    ) * (1.0 / math.sqrt(HD))
    query_pos = offset + lax.iota(jnp.int32, block_rows)
    key_pos = lax.iota(jnp.int32, key_rows.shape[0])
    block_docs = doc_rows[offset : offset + block_rows]
    allowed = (block_docs[:, None] == doc_rows[None, :]) & (query_pos[:, None] >= key_pos[None, :])
    return jnp.where(allowed[None], scores, -1e30)


def attend_forward(queries, key_rows, value_rows, doc_rows):
    seq_len = queries.shape[0]
    block_rows = min(512, seq_len)
    outputs = []
    log_parts = []
    for offset in range(0, seq_len, block_rows):
        scores = block_scores(queries[offset : offset + block_rows], key_rows, doc_rows, offset)
        row_max = jnp.max(scores, axis=-1, keepdims=True)
        log_total = row_max + jnp.log(jnp.sum(jnp.exp(scores - row_max), axis=-1, keepdims=True))
        probabilities = jnp.exp(scores - log_total).astype(jnp.bfloat16)
        outputs.append(
            jnp.einsum(
                "hqk,khd->qhd", probabilities, value_rows, preferred_element_type=jnp.float32
            )
        )
        log_parts.append(log_total[..., 0])
    return (jnp.concatenate(outputs, axis=0), jnp.concatenate(log_parts, axis=1))


def attend_backward(queries, key_rows, value_rows, doc_rows, log_totals, grad_out):
    seq_len = queries.shape[0]
    block_rows = min(512, seq_len)
    scale_factor = 1.0 / math.sqrt(HD)
    grad_queries = []
    grad_keys = jnp.zeros(key_rows.shape, jnp.float32)
    grad_values = jnp.zeros(value_rows.shape, jnp.float32)
    for offset in range(0, seq_len, block_rows):
        query_block = queries[offset : offset + block_rows]
        grad_block = grad_out[offset : offset + block_rows]
        scores = block_scores(query_block, key_rows, doc_rows, offset)
        probabilities = jnp.exp(scores - log_totals[:, offset : offset + block_rows, None])
        grad_probs = jnp.einsum(
            "qhd,khd->hqk", grad_block, value_rows, preferred_element_type=jnp.float32
        )
        row_dots = jnp.sum(probabilities * grad_probs, axis=-1, keepdims=True)
        grad_scores = (probabilities * (grad_probs - row_dots)).astype(jnp.bfloat16)
        grad_queries.append(
            scale_factor
            * jnp.einsum("hqk,khd->qhd", grad_scores, key_rows, preferred_element_type=jnp.float32)
        )
        grad_keys = grad_keys + scale_factor * jnp.einsum(
            "hqk,qhd->khd", grad_scores, query_block, preferred_element_type=jnp.float32
        )
        grad_values = grad_values + jnp.einsum(
            "hqk,qhd->khd",
            probabilities.astype(jnp.bfloat16),
            grad_block,
            preferred_element_type=jnp.float32,
        )
    return (jnp.concatenate(grad_queries, axis=0), grad_keys, grad_values)


def swap_mp(x):
    return lax.ppermute(x, "mp", [(0, 1), (1, 0)])


def row_halves(x, m):
    half = x.shape[0] // 2
    own = lax.dynamic_slice_in_dim(x, m * half, half, axis=0)
    other = lax.dynamic_slice_in_dim(x, (1 - m) * half, half, axis=0)
    return own, other


def join_pair(own, other, m, axis):
    return jnp.where(
        m == 0,
        jnp.concatenate([own, other], axis=axis),
        jnp.concatenate([other, own], axis=axis),
    )


def scatter_rows_mp(partial, m, send_dtype):
    own, other = row_halves(partial, m)
    return own + swap_mp(other.astype(send_dtype)).astype(own.dtype)


def gather_rows_mp(own, m):
    return join_pair(own, swap_mp(own), m, 0)


def scatter_dp(x, ndp):
    idx = lax.axis_index("dp")
    bits = ndp.bit_length() - 1
    chunk = x.shape[0] // ndp
    rest = x.shape[1:]
    cur = x.reshape((2,) * bits + (chunk,) + rest)
    remaining = list(range(bits - 1, -1, -1))
    for bit in range(bits):
        pos = remaining.index(bit)
        mine = (idx >> bit) & 1
        keep = lax.dynamic_index_in_dim(cur, mine, pos, keepdims=False)
        send = lax.dynamic_index_in_dim(cur, 1 - mine, pos, keepdims=False)
        got = lax.ppermute(send, "dp", [(i, i ^ (1 << bit)) for i in range(ndp)])
        cur = keep + got
        remaining.pop(pos)
    return cur.reshape((chunk,) + rest)


def reduce_tree(x, name, size):
    bits = size.bit_length() - 1
    for bit in range(bits):
        x = x + lax.ppermute(x, name, [(i, i ^ (1 << bit)) for i in range(size)])
    return x


def make_shards(ndp, nmp):
    def shards(
        tokens,
        doc_ids,
        ln1_gain,
        ln1_bias,
        w_qkv,
        b_qv,
        w_out,
        b_out,
        ln2_gain,
        ln2_bias,
        w_up,
        b_up,
        w_down,
        b_down,
        cotangent,
    ):
        m = lax.axis_index("mp")
        row_count = tokens.shape[0]
        local_width = w_qkv.shape[2]
        seq_count, seq_len = doc_ids.shape
        seq_shape = (seq_count, seq_len, local_width // HD, HD)
        token_rows = tokens.astype(jnp.float32)
        normal_one, inv_one = normalize(token_rows)
        gain_one = ln1_gain.astype(jnp.float32)
        normed_one = (normal_one * gain_one + ln1_bias.astype(jnp.float32)).astype(jnp.bfloat16)
        projected = jnp.einsum(
            "td,dce->tce", normed_one, w_qkv, preferred_element_type=jnp.float32
        )
        bias_qv = b_qv.astype(jnp.float32)
        queries = (projected[:, 0] + bias_qv[0]).astype(jnp.bfloat16).reshape(seq_shape)
        key_rows = projected[:, 1].astype(jnp.bfloat16).reshape(seq_shape)
        value_rows = (projected[:, 2] + bias_qv[1]).astype(jnp.bfloat16).reshape(seq_shape)
        attended = []
        log_totals = []
        for s in range(seq_count):
            out_s, lse_s = attend_forward(queries[s], key_rows[s], value_rows[s], doc_ids[s])
            attended.append(out_s)
            log_totals.append(lse_s)
        mixed = jnp.stack(attended).reshape(row_count, local_width).astype(jnp.bfloat16)
        mixed_all = join_pair(mixed, swap_mp(mixed), m, 1)
        w_out_all = join_pair(w_out, swap_mp(w_out), m, 0)
        attn_all = jnp.dot(mixed_all, w_out_all, preferred_element_type=jnp.float32)
        after_attn = token_rows + attn_all + b_out.astype(jnp.float32)
        gain_two = ln2_gain.astype(jnp.float32)
        normal_two, inv_two = normalize(after_attn)
        normed_two = (normal_two * gain_two + ln2_bias.astype(jnp.float32)).astype(jnp.bfloat16)
        up_rows = jnp.dot(normed_two, w_up, preferred_element_type=jnp.float32) + b_up.astype(
            jnp.float32
        )
        activated, gelu_pull = jax.vjp(gelu_tanh, up_rows)
        act_rows = activated.astype(jnp.bfloat16)
        ffn_part = jnp.dot(act_rows, w_down, preferred_element_type=jnp.float32)
        ffn_own = scatter_rows_mp(ffn_part, m, jnp.bfloat16)
        after_own, _ = row_halves(after_attn, m)
        out_own = (after_own + (ffn_own + b_down.astype(jnp.float32))).astype(jnp.bfloat16)
        block_out = gather_rows_mp(out_own, m)

        cot_rows = cotangent.astype(jnp.float32)
        cot_own, _ = row_halves(cot_rows, m)
        grad_w_down_t = jnp.einsum(
            "td,tf->df", cotangent, act_rows, preferred_element_type=jnp.float32
        )
        grad_act = jnp.einsum("td,fd->tf", cotangent, w_down, preferred_element_type=jnp.float32)
        grad_up = gelu_pull(grad_act)[0].astype(jnp.bfloat16)
        grad_w_up = jnp.einsum("td,tf->df", normed_two, grad_up, preferred_element_type=jnp.float32)
        grad_b_up = jnp.sum(grad_up.astype(jnp.float32), axis=0)
        norm_two_part = jnp.einsum("tf,df->td", grad_up, w_up, preferred_element_type=jnp.float32)
        grad_two_own = scatter_rows_mp(norm_two_part, m, jnp.float32)
        normal_two_own, _ = row_halves(normal_two, m)
        inv_two_own, _ = row_halves(inv_two, m)
        grad_after_own = cot_own + norm_back(grad_two_own, normal_two_own, inv_two_own, gain_two)
        grad_attn_own = grad_after_own.astype(jnp.bfloat16)
        grad_attn_here = gather_rows_mp(grad_attn_own, m)
        grad_w_out_t = jnp.einsum(
            "td,te->de", grad_attn_here, mixed, preferred_element_type=jnp.float32
        )
        grad_mixed = jnp.einsum(
            "td,ed->te", grad_attn_here, w_out, preferred_element_type=jnp.float32
        ).astype(jnp.bfloat16)
        grad_mixed = grad_mixed.reshape(seq_shape)
        gq, gk, gv = [], [], []
        for s in range(seq_count):
            dq_s, dk_s, dv_s = attend_backward(
                queries[s], key_rows[s], value_rows[s], doc_ids[s], log_totals[s], grad_mixed[s]
            )
            gq.append(dq_s)
            gk.append(dk_s)
            gv.append(dv_s)
        grad_q = jnp.stack(gq).reshape(row_count, local_width).astype(jnp.bfloat16)
        grad_k = jnp.stack(gk).reshape(row_count, local_width).astype(jnp.bfloat16)
        grad_v = jnp.stack(gv).reshape(row_count, local_width).astype(jnp.bfloat16)
        grad_proj = jnp.stack([grad_q, grad_k, grad_v], axis=1)
        grad_w_qkv = jnp.einsum(
            "td,tce->dce", normed_one, grad_proj, preferred_element_type=jnp.float32
        )
        grad_b_qv = jnp.stack(
            [
                jnp.sum(grad_q.astype(jnp.float32), axis=0),
                jnp.sum(grad_v.astype(jnp.float32), axis=0),
            ]
        )
        norm_one_part = jnp.einsum(
            "tce,dce->td", grad_proj, w_qkv, preferred_element_type=jnp.float32
        )
        grad_one_own = scatter_rows_mp(norm_one_part, m, jnp.float32)
        normal_one_own, _ = row_halves(normal_one, m)
        inv_one_own, _ = row_halves(inv_one, m)
        grad_input_own = grad_after_own + norm_back(
            grad_one_own, normal_one_own, inv_one_own, gain_one
        )
        grad_input = gather_rows_mp(grad_input_own, m)
        vector_terms = jnp.stack(
            [
                jnp.sum(grad_one_own * normal_one_own, axis=0),
                jnp.sum(grad_one_own, axis=0),
                jnp.sum(grad_two_own * normal_two_own, axis=0),
                jnp.sum(grad_two_own, axis=0),
                jnp.sum(grad_attn_own.astype(jnp.float32), axis=0),
                jnp.sum(cot_own, axis=0),
            ]
        )
        n_vec = vector_terms.size
        n_qv = grad_b_qv.size
        packed = jnp.concatenate([vector_terms.reshape(-1), grad_b_qv.reshape(-1), grad_b_up])
        packed = reduce_tree(packed, "dp", ndp)
        vector_sum = reduce_tree(packed[:n_vec], "mp", nmp).reshape(vector_terms.shape)
        qv_sum = packed[n_vec : n_vec + n_qv].reshape(grad_b_qv.shape)
        up_sum = packed[n_vec + n_qv :]
        sum_qkv = scatter_dp(grad_w_qkv, ndp)
        sum_out = scatter_dp(grad_w_out_t, ndp).T
        sum_up = scatter_dp(grad_w_up, ndp)
        sum_down = scatter_dp(grad_w_down_t, ndp).T
        return (
            block_out,
            grad_input,
            vector_sum[0],
            vector_sum[1],
            sum_qkv,
            qv_sum,
            sum_out,
            vector_sum[4],
            vector_sum[2],
            vector_sum[3],
            sum_up,
            up_sum,
            sum_down,
            vector_sum[5],
        )

    return shards


def solution(mesh):
    return jax.shard_map(
        make_shards(mesh.shape["dp"], mesh.shape["mp"]),
        mesh=mesh,
        in_specs=(
            P("dp", None),
            P("dp", None),
            P(),
            P(),
            P(None, None, "mp"),
            P(None, "mp"),
            P("mp", None),
            P(),
            P(),
            P(),
            P(None, "mp"),
            P("mp"),
            P("mp", None),
            P(),
            P("dp", None),
        ),
        out_specs=(
            P("dp", None),
            P("dp", None),
            P(),
            P(),
            P("dp", None, "mp"),
            P(None, "mp"),
            P("mp", "dp"),
            P(),
            P(),
            P(),
            P("dp", "mp"),
            P("mp"),
            P("mp", "dp"),
            P(),
        ),
        check_vma=False,
    )
```

time: 778 us -> 416 us (0.53)
  waiting for transfers between devices: 492 us -> 146 us
  blocking collectives: 61.8 us -> 0 us
  local copies, waits for them, and re-layouts: 17.3 us -> 51.9 us
  starting transfers between devices: 0.58 us -> 29.4 us
  matrix products: 124 us -> 103 us
  other arithmetic: 62.7 us -> 79.4 us
  between operations: 15.2 us -> 2.09 us
    psum x4 -> x0, waiting for transfers between devices: 270 us -> none  [the longest x1 83.5 us: shards(): lax.psum(attn_part, 'mp')]
    reduce_scatter x4 -> x0, waiting for transfers between devices: 222 us -> none  [the longest x1 79.2 us: shards(): lax.psum_scatter(grad_w_up, 'dp', scatter_dimension=0, tiled=True)]
    ppermute x0 -> x29, waiting for transfers between devices: none -> 146 us  [the longest x8 75.9 us: swap_mp(): return lax.ppermute(x, 'mp', [(0, 1), (1, 0)])]
    psum x1 -> x0, blocking collectives: 61.8 us -> none  [shards(): lax.psum((vector_terms, grad_b_qv, grad_b_up), 'dp')]
    ppermute x0 -> x29, starting transfers between devices: none -> 29.4 us  [the longest x16 15.2 us: scatter_dp(): got = lax.ppermute(send, 'dp', [(i, i ^ 1 << bit) for i in range(ndp)])]
    dynamic_slice x0 -> x7, local copies, waits for them, and re-layouts: none -> 14 us  [the longest x3 6.23 us: scatter_dp(): send = lax.dynamic_index_in_dim(cur, 1 - mine, pos, keepdims=False)]
    add x1 -> x20, other arithmetic: 5.15 us -> 18 us  [the longest x14 15 us: scatter_dp(): cur = keep + got]
  transfers between devices with their start and end apart: 8 -> 29, of which waited for: 7 -> 13; matrix products, arithmetic and copies ran while one was open for 6% -> 38% of each run, Pallas kernels for 0% -> 0%
where the time goes in v1:
time: 416 us; the launch traced here: 412 us
  waiting for transfers between devices  146 us (35%)
  matrix products  103 us (25%)
  other arithmetic  79.4 us (19%)
  local copies, waits for them, and re-layouts  51.9 us (12%)
  starting transfers between devices  29.4 us (7%)
    ppermute x8, waiting for transfers between devices, swap_mp(): return lax.ppermute(x, 'mp', [(0, 1), (1, 0)])  75.9 us
    ppermute x16, waiting for transfers between devices, scatter_dp(): got = lax.ppermute(send, 'dp', [(i, i ^ 1 << bit) for i in range(ndp)])  52.8 us
    dot_general x2, matrix products, attend_backward(): jnp.einsum('qhd,khd->hqk', grad_block, value_rows, preferred_element_type...  20.5 us
    convert_element_type x1, other arithmetic, attend_backward(): grad_scores = (probabilities * (grad_probs - row_dots)).astype(jnp.bfloat16)  17.8 us
    ppermute x5, waiting for transfers between devices, reduce_tree(): x = x + lax.ppermute(x, name, [(i, i ^ 1 << bit) for i in range(size)])  17.6 us
    ppermute x16, starting transfers between devices, scatter_dp(): got = lax.ppermute(send, 'dp', [(i, i ^ 1 << bit) for i in range(ndp)])  15.2 us
    add x14, other arithmetic, scatter_dp(): cur = keep + got  15 us
    unnamed x176, local copies, waits for them, and re-layouts  12.9 us
  transfers between devices with their start and end apart: 29, of which 13 were waited for; matrix products, arithmetic and copies ran while one was open for 38% of the time, Pallas kernels for 0%

profile of v1, /device:TPU:0, one launch (start us, length us, event | category | flops | bytes accessed | tf_op | source)
XLA Modules:
  0.0 412.1 jit_solution(17886813715169542518)
XLA Ops:
  6.5 3.9 fusion.43
  18.9 3.6 exponential_reduce_fusion.1
  25.0 3.6 exponential_reduce_fusion
  33.5 8.0 %convolution_convert_fusion.1 = bf16[6,64,512]{2,1,0:T(8,128)(2,1)S(1)} fusion(bf16[1024,6,64]{0,2,1:T(8,128)(2,1)S(1)} %add_convert_fusion.4, f32[6,512,1024]{2,1,0:T(8,128)} %copy-done.3, f32[6,512]{1,0:T(8,128)S(1)} %log_add_fusion, pred[512,1024]{1,0:T(8,128)(4,1)S(1)} %get-tuple-element.52), kind=kOutput, calls=%fused_computation.89 | convolution fusion | flops 415432704 | bytes 14299136 | tf_op jit(solution)/shard_map/hqk,khd->qhd/dot_general | solution.py:62
  51.8 27.2 %collective-permute-done.1 = bf16[384,768]{1,0:T(8,128)(2,1)} collective-permute-done((bf16[384,768]{1,0:T(8,128)(2,1)}, bf16[384,768]{1,0:T(8,128)(2,1)}, u32[]{:S(2)}, u32[]{:S(2)}) %collective-permute-start.1) | collective-permute-done | bytes 589856 | tf_op jit(solution)/shard_map/ppermute | solution.py:104
  79.0 4.7 %fusion.62 = (f32[1024]{0:T(1024)S(1)}, f32[1024,768]{1,0:T(8,128)S(1)}) fusion(f32[768]{0:T(1024)} %convert_element_type.163, bf16[384,768]{1,0:T(8,128)(2,1)} %collective-permute-done.1, bf16[384,768]{1,0:T(8,128)(2,1)} %param.21, pred[]{:T(512)S(6)} %eq.24, bf16[1024,384]{1,0:T(8,128)(2,1)} %collective-permute-done, bf16[1024,384]{1,0:T(8,128)(2,1)} %copy.59, ...), kind=kOutput, calls=%fused_computation.170 | convolution fusion | flops 1223490560 | bytes 7478273 | tf_op jit(solution)/shard_map/dot_general | solution.py:199
  89.7 9.5 %convert_reduce_fusion = (f32[1536]{0:T(1024)}, bf16[1024,1536]{1,0:T(8,128)(2,1)S(1)}, bf16[1024,1536]{1,0:T(8,128)(2,1)S(1)}) fusion(f32[1024,1536]{1,0:T(8,128)S(1)} %fusion.38, f32[1536]{0:T(1024)S(1)} %copy-done.72, bf16[1024,768]{1,0:T(8,128)(2,1)S(1)} %copy-done.54, bf16[1536,768]{1,0:T(8,128)(2,1)S(1)} %copy-done), kind=kOutput, calls=%fused_computation.24 | convolution fusion | flops 2461530624 | bytes 16527360 | tf_op jit(solution)/shard_map/td,fd->tf/dot_general | solution.py:220
  116.3 5.7 %fusion.37 = f32[768,1536]{1,0:T(8,128)S(1)} fusion(bf16[1024,1536]{1,0:T(8,128)(2,1)} %copy-done.34, f32[1024,768]{1,0:T(8,128)} %copy-done.5, f32[768]{0:T(1024)S(1)} %convert_element_type.165, f32[768]{0:T(1024)S(1)} %convert_element_type.164), kind=kOutput, calls=%fused_computation.118 | convolution fusion | flops 2418278400 | bytes 11016192 | tf_op jit(solution)/shard_map/td,tf->df/dot_general | solution.py:222
  122.0 33.8 %collective-permute-done.2 = bf16[512,768]{1,0:T(8,128)(2,1)S(1)} collective-permute-done((bf16[512,768]{1,0:T(8,128)(2,1)S(1)}, bf16[512,768]{1,0:T(8,128)(2,1)S(1)}, u32[]{:S(2)}, u32[]{:S(2)}) %collective-permute-start.2) | collective-permute-done | bytes 786464 | tf_op jit(solution)/shard_map/ppermute | solution.py:104
  178.4 12.5 %collective-permute-done.5 = bf16[512,768]{1,0:T(8,128)(2,1)S(1)} collective-permute-done((bf16[512,768]{1,0:T(8,128)(2,1)S(1)}, bf16[512,768]{1,0:T(8,128)(2,1)S(1)}, u32[]{:S(2)}, u32[]{:S(2)}) %collective-permute-start.5) | collective-permute-done | bytes 786464 | tf_op jit(solution)/shard_map/ppermute | solution.py:104
  199.1 6.6 %fusion.52 = f32[6,64,1024]{2,1,0:T(8,128)S(1)} fusion(bf16[512,6,64]{0,2,1:T(8,128)(2,1)S(1)} %bitcast.188, f32[6,512,1024]{2,1,0:T(8,128)} %copy-done.2, f32[6,512]{1,0:T(8,128)S(1)} %copy-done.60, pred[512,1024]{1,0:T(8,128)(4,1)S(1)} %copy-done.13), kind=kOutput, calls=%fused_computation.165 | convolution fusion | flops 415236096 | bytes 15085568 | tf_op jit(solution)/shard_map/hqk,qhd->khd/dot_general | solution.py:94
  206.3 4.8 %convert_reduce_fusion.3 = (f32[6,64]{1,0:T(8,128)S(1)}, bf16[6,64,1024]{2,1,0:T(8,128)(2,1)}) fusion(f32[6,64,1024]{2,1,0:T(8,128)S(1)} %fusion.52, bf16[512,6,64]{0,2,1:T(8,128)(2,1)S(1)} %bitcast.190, f32[6,512,1024]{2,1,0:T(8,128)S(1)} %bitcast.165, f32[6,512]{1,0:T(8,128)S(1)} %copy-done.62, pred[512,1024]{1,0:T(8,128)(4,1)S(1)} %copy-done.15), kind=kOutput, calls=%fused_computation.66 | convolution fusion | flops 416808576 | bytes 15873536 | tf_op jit(solution)/shard_map/hqk,qhd->khd/dot_general | solution.py:94
  213.4 10.4 %multiply_reduce_fusion = (f32[6,512]{1,0:T(8,128)S(1)}, f32[6,512,1024]{2,1,0:T(8,128)}) fusion(f32[6,512,1024]{2,1,0:T(8,128)} %copy-done.3, f32[6,512]{1,0:T(8,128)S(1)} %copy-done.62, pred[512,1024]{1,0:T(8,128)(4,1)S(1)} %copy-done.15, bf16[512,6,64]{0,2,1:T(8,128)(2,1)} %bitcast.191, bf16[1024,6,64]{0,2,1:T(8,128)(2,1)S(1)} %copy-done.24), kind=kOutput, calls=%fused_computation.1 | convolution fusion | flops 418378752 | bytes 26894336 | tf_op jit(solution)/shard_map/qhd,khd->hqk/dot_general | solution.py:82
  223.9 10.0 %multiply_reduce_fusion.1 = (f32[6,512]{1,0:T(8,128)S(1)}, f32[6,512,1024]{2,1,0:T(8,128)}) fusion(f32[6,512,1024]{2,1,0:T(8,128)} %copy-done.2, f32[6,512]{1,0:T(8,128)S(1)} %copy-done.60, pred[512,1024]{1,0:T(8,128)(4,1)S(1)} %copy-done.13, bf16[512,6,64]{0,2,1:T(8,128)(2,1)S(1)} %bitcast.189, bf16[1024,6,64]{0,2,1:T(8,128)(2,1)S(1)} %copy-done.24), kind=kOutput, calls=%fused_computation.3 | convolution fusion | flops 418378752 | bytes 26894336 | tf_op jit(solution)/shard_map/qhd,khd->hqk/dot_general | solution.py:82
  239.7 17.8 %multiply_convert_fusion = (bf16[6,512,1024]{2,1,0:T(8,128)(2,1)}, bf16[6,512,1024]{2,1,0:T(8,128)(2,1)}) fusion(f32[6,512,1024]{2,1,0:T(8,128)} %get-tuple-element.64, f32[6,512,1024]{2,1,0:T(8,128)} %copy-done.3, f32[6,512]{1,0:T(8,128)S(1)} %get-tuple-element.63, f32[6,512]{1,0:T(8,128)S(1)} %copy-done.62, pred[512,1024]{1,0:T(8,128)(4,1)S(1)} %copy-done.15, ...), kind=kLoop, calls=%fused_computation | loop fusion | flops 37748736 | bytes 64012288 | tf_op jit(solution)/shard_map/convert_element_type | solution.py:86
  257.5 4.1 %fusion.65 = f32[6,64,1024]{2,1,0:T(8,128)S(1)} fusion(bf16[512,6,64]{0,2,1:T(8,128)(2,1)S(1)} %bitcast.178, bf16[6,512,1024]{2,1,0:T(8,128)(2,1)} %get-tuple-element.68), kind=kOutput, calls=%fused_computation.173 | convolution fusion | flops 402653184 | bytes 8257536 | tf_op jit(solution)/shard_map/hqk,qhd->khd/dot_general | solution.py:91
  274.2 4.0 convolution_bitcast_fusion
  287.1 14.7 %collective-permute-done.18 = f32[2,2,48,384]{3,2,1,0:T(8,128)S(1)} collective-permute-done((f32[2,2,48,384]{3,2,1,0:T(8,128)S(1)}, f32[2,2,48,384]{3,2,1,0:T(8,128)S(1)}, u32[]{:S(2)}, u32[]{:S(2)}) %collective-permute-start.18) | collective-permute-done | bytes 294944 | tf_op jit(solution)/shard_map/ppermute | solution.py:143
  317.7 4.0 multiply_reduce_fusion.4
  332.7 13.7 %collective-permute-done.10 = f32[6912]{0:T(1024)S(1)} collective-permute-done((f32[6912]{0:T(1024)S(1)}, f32[6912]{0:T(1024)S(1)}, u32[]{:S(2)}, u32[]{:S(2)}) %collective-permute-start.10) | collective-permute-done | bytes 27680 | tf_op jit(solution)/shard_map/ppermute | solution.py:152
  367.0 13.3 %collective-permute-done.14 = f32[2,2,48,3,384]{4,2,3,1,0:T(8,128)S(1)} collective-permute-done((f32[2,2,48,3,384]{4,2,3,1,0:T(8,128)S(1)}, f32[2,2,48,3,384]{4,2,3,1,0:T(8,128)S(1)}, u32[]{:S(2)}, u32[]{:S(2)}) %collective-permute-start.14) | collective-permute-done | bytes 884768 | tf_op jit(solution)/shard_map/ppermute | solution.py:143
  383.5 14.9 %collective-permute-done.15 = f32[2,48,3,384]{3,1,2,0:T(8,128)S(1)} collective-permute-done((f32[2,48,3,384]{3,1,2,0:T(8,128)S(1)}, f32[2,48,3,384]{3,1,2,0:T(8,128)S(1)}, u32[]{:S(2)}, u32[]{:S(2)}) %collective-permute-start.15) | collective-permute-done | bytes 442400 | tf_op jit(solution)/shard_map/ppermute | solution.py:143
  399.5 5.0 %maximum_select_fusion = f32[1024,768]{1,0:T(8,128)} fusion(f32[512,768]{1,0:T(8,128)} %collective-permute-done.7, f32[512,768]{1,0:T(8,128)} %multiply_add_fusion.2, pred[]{:T(512)S(6)} %eq.24), kind=kLoop, calls=%fused_computation.33 | loop fusion | flops 2359296 | bytes 6291457 | tf_op jit(solution)/shard_map/jit(_where)/select_n | solution.py:115
  404.5 6.6 %collective-permute-done.16 = f32[48,3,384]{2,0,1:T(8,128)S(1)} collective-permute-done((f32[48,3,384]{2,0,1:T(8,128)S(1)}, f32[48,3,384]{2,0,1:T(8,128)S(1)}, u32[]{:S(2)}, u32[]{:S(2)}) %collective-permute-start.16) | collective-permute-done | bytes 221216 | tf_op jit(solution)/shard_map/ppermute | solution.py:143
  (354 shorter events, 167.8 us)
Async XLA Ops:
  45.5 33.5 %collective-permute-start = (bf16[1024,384]{1,0:T(8,128)(2,1)}, bf16[1024,384]{1,0:T(8,128)(2,1)}, u32[]{:S(2)}, u32[]{:S(2)}) collective-permute-start(bf16[1024,384]{1,0:T(8,128)(2,1)} %copy.59), channel_id=1, source_target_pairs={{0,1},{1,0},{2,3},{3,2},{4,5},{5,4},{6,7},{7,6},{8,9},{9,8},{10,11... | collective-permute-start | bytes 2359304 | tf_op jit(solution)/shard_map/ppermute | solution.py:104
  48.5 30.5 %collective-permute-start.1 = (bf16[384,768]{1,0:T(8,128)(2,1)}, bf16[384,768]{1,0:T(8,128)(2,1)}, u32[]{:S(2)}, u32[]{:S(2)}) collective-permute-start(bf16[384,768]{1,0:T(8,128)(2,1)} %param.21), channel_id=1, source_target_pairs={{0,1},{1,0},{2,3},{3,2},{4,5},{5,4},{6,7},{7,6},{8,9},{9,8},{10,11... | collective-permute-start | bytes 1769480 | tf_op jit(solution)/shard_map/ppermute | solution.py:104
  103.2 54.5 %collective-permute-start.4 = (f32[512,768]{1,0:T(8,128)}, f32[512,768]{1,0:T(8,128)}, u32[]{:S(2)}, u32[]{:S(2)}) collective-permute-start(f32[512,768]{1,0:T(8,128)} %constant_dynamic-slice_fusion.7), channel_id=1, source_target_pairs={{0,1},{1,0},{2,3},{3,2},{4,5},{5,4},{6,7},{7,6},{8,9},{9,8},{10,11... | collective-permute-start | bytes 4718600 | tf_op jit(solution)/shard_map/ppermute | solution.py:104
  109.2 46.6 %collective-permute-start.2 = (bf16[512,768]{1,0:T(8,128)(2,1)S(1)}, bf16[512,768]{1,0:T(8,128)(2,1)S(1)}, u32[]{:S(2)}, u32[]{:S(2)}) collective-permute-start(bf16[512,768]{1,0:T(8,128)(2,1)S(1)} %dynamic-slice_convert_fusion), channel_id=1, source_target_pairs={{0,1},{1,0},{2,3},{3,2},{4,5},{5,4},{6,7},{7,6},{8,9},{9,8},{10,11... | collective-permute-start | bytes 2359304 | tf_op jit(solution)/shard_map/ppermute | solution.py:104
  156.1 20.5 %collective-permute-start.3 = (bf16[512,768]{1,0:T(8,128)(2,1)S(1)}, bf16[512,768]{1,0:T(8,128)(2,1)S(1)}, u32[]{:S(2)}, u32[]{:S(2)}) collective-permute-start(bf16[512,768]{1,0:T(8,128)(2,1)S(1)} %add_convert_fusion.3), channel_id=1, source_target_pairs={{0,1},{1,0},{2,3},{3,2},{4,5},{5,4},{6,7},{7,6},{8,9},{9,8},{10,11... | collective-permute-start | bytes 2359304 | tf_op jit(solution)/shard_map/ppermute | solution.py:104
  161.6 29.3 %collective-permute-start.5 = (bf16[512,768]{1,0:T(8,128)(2,1)S(1)}, bf16[512,768]{1,0:T(8,128)(2,1)S(1)}, u32[]{:S(2)}, u32[]{:S(2)}) collective-permute-start(bf16[512,768]{1,0:T(8,128)(2,1)S(1)} %get-tuple-element.25), channel_id=1, source_target_pairs={{0,1},{1,0},{2,3},{3,2},{4,5},{5,4},{6,7},{7,6},{8,9},{9,8},{10,11... | collective-permute-start | bytes 2359304 | tf_op jit(solution)/shard_map/ppermute | solution.py:104
  171.4 62.5 %collective-permute-start.21 = (f32[2,2,2,48,1536]{4,3,1,0,2:T(8,128)}, f32[2,2,2,48,1536]{4,3,1,0,2:T(8,128)}, u32[]{:S(2)}, u32[]{:S(2)}) collective-permute-start(f32[2,2,2,48,1536]{4,3,1,0,2:T(8,128)} %bitcast.160), channel_id=1, source_target_pairs={{0,2},{2,0},{4,6},{6,4},{8,10},{10,8},{12,14},{14,12},{16,18},{18,... | collective-permute-start | bytes 7077896 | tf_op jit(solution)/shard_map/ppermute | solution.py:143
  171.4 92.8 %collective-permute-start.25 = (f32[2,2,2,48,1536]{4,3,1,0,2:T(8,128)}, f32[2,2,2,48,1536]{4,3,1,0,2:T(8,128)}, u32[]{:S(2)}, u32[]{:S(2)}) collective-permute-start(f32[2,2,2,48,1536]{4,3,1,0,2:T(8,128)} %bitcast.159), channel_id=1, source_target_pairs={{0,2},{2,0},{4,6},{6,4},{8,10},{10,8},{12,14},{14,12},{16,18},{18,... | collective-permute-start | bytes 7077896 | tf_op jit(solution)/shard_map/ppermute | solution.py:143
  198.7 82.0 %collective-permute-start.17 = (f32[2,2,2,48,384]{4,3,2,1,0:T(8,128)}, f32[2,2,2,48,384]{4,3,2,1,0:T(8,128)}, u32[]{:S(2)}, u32[]{:S(2)}) collective-permute-start(f32[2,2,2,48,384]{4,3,2,1,0:T(8,128)} %dynamic-slice_bitcast_fusion.5), channel_id=1, source_target_pairs={{0,2},{2,0},{4,6},{6,4},{8,10},{10,8},{12,14},{14,12},{16,18},{18,... | collective-permute-start | bytes 1769480 | tf_op jit(solution)/shard_map/ppermute | solution.py:143
  238.5 74.9 %collective-permute-start.22 = (f32[2,2,48,1536]{3,2,1,0:T(8,128)}, f32[2,2,48,1536]{3,2,1,0:T(8,128)}, u32[]{:S(2)}, u32[]{:S(2)}) collective-permute-start(f32[2,2,48,1536]{3,2,1,0:T(8,128)} %dynamic-slice_bitcast_fusion.1), channel_id=1, source_target_pairs={{0,4},{2,6},{4,0},{6,2},{8,12},{10,14},{12,8},{14,10},{16,20},{18,... | collective-permute-start | bytes 3538952 | tf_op jit(solution)/shard_map/ppermute | solution.py:143
  267.6 58.8 %collective-permute-start.26 = (f32[2,2,48,1536]{3,2,1,0:T(8,128)}, f32[2,2,48,1536]{3,2,1,0:T(8,128)}, u32[]{:S(2)}, u32[]{:S(2)}) collective-permute-start(f32[2,2,48,1536]{3,2,1,0:T(8,128)} %dynamic-slice_bitcast_fusion), channel_id=1, source_target_pairs={{0,4},{2,6},{4,0},{6,2},{8,12},{10,14},{12,8},{14,10},{16,20},{18,... | collective-permute-start | bytes 3538952 | tf_op jit(solution)/shard_map/ppermute | solution.py:143
  279.6 38.1 %collective-permute-start.6 = (f32[512,768]{1,0:T(8,128)}, f32[512,768]{1,0:T(8,128)}, u32[]{:S(2)}, u32[]{:S(2)}) collective-permute-start(f32[512,768]{1,0:T(8,128)} %constant_dynamic-slice_fusion.6), channel_id=1, source_target_pairs={{0,1},{1,0},{2,3},{3,2},{4,5},{5,4},{6,7},{7,6},{8,9},{9,8},{10,11... | collective-permute-start | bytes 4718600 | tf_op jit(solution)/shard_map/ppermute | solution.py:104
  282.2 19.6 %collective-permute-start.18 = (f32[2,2,48,384]{3,2,1,0:T(8,128)S(1)}, f32[2,2,48,384]{3,2,1,0:T(8,128)S(1)}, u32[]{:S(2)}, u32[]{:S(2)}) collective-permute-start(f32[2,2,48,384]{3,2,1,0:T(8,128)S(1)} %dynamic-slice_bitcast_fusion.9), channel_id=1, source_target_pairs={{0,4},{2,6},{4,0},{6,2},{8,12},{10,14},{12,8},{14,10},{16,20},{18,... | collective-permute-start | bytes 884744 | tf_op jit(solution)/shard_map/ppermute | solution.py:143
  312.8 45.6 %collective-permute-start.13 = (f32[2,2,2,48,3,384]{5,3,4,2,1,0:T(8,128)}, f32[2,2,2,48,3,384]{5,3,4,2,1,0:T(8,128)}, u32[]{:S(2)}, u32[]{:S(2)}) collective-permute-start(f32[2,2,2,48,3,384]{5,3,4,2,1,0:T(8,128)} %bitcast.161), channel_id=1, source_target_pairs={{0,2},{2,0},{4,6},{6,4},{8,10},{10,8},{12,14},{14,12},{16,18},{18,... | collective-permute-start | bytes 5308424 | tf_op jit(solution)/shard_map/ppermute | solution.py:143
  316.1 45.5 %collective-permute-start.23 = (f32[2,48,1536]{2,1,0:T(8,128)}, f32[2,48,1536]{2,1,0:T(8,128)}, u32[]{:S(2)}, u32[]{:S(2)}) collective-permute-start(f32[2,48,1536]{2,1,0:T(8,128)} %dynamic-slice_bitcast_fusion.4), channel_id=1, source_target_pairs={{0,8},{2,10},{4,12},{6,14},{8,0},{10,2},{12,4},{14,6},{16,24},{18,... | collective-permute-start | bytes 1769480 | tf_op jit(solution)/shard_map/ppermute | solution.py:143
  329.9 35.2 %collective-permute-start.27 = (f32[2,48,1536]{2,1,0:T(8,128)}, f32[2,48,1536]{2,1,0:T(8,128)}, u32[]{:S(2)}, u32[]{:S(2)}) collective-permute-start(f32[2,48,1536]{2,1,0:T(8,128)} %dynamic-slice_bitcast_fusion.3), channel_id=1, source_target_pairs={{0,8},{2,10},{4,12},{6,14},{8,0},{10,2},{12,4},{14,6},{16,24},{18,... | collective-permute-start | bytes 1769480 | tf_op jit(solution)/shard_map/ppermute | solution.py:143
  332.0 14.4 %collective-permute-start.10 = (f32[6912]{0:T(1024)S(1)}, f32[6912]{0:T(1024)S(1)}, u32[]{:S(2)}, u32[]{:S(2)}) collective-permute-start(f32[6912]{0:T(1024)S(1)} %add.326), channel_id=1, source_target_pairs={{0,8},{2,10},{4,12},{6,14},{8,0},{10,2},{12,4},{14,6},{16,24},{18,... | collective-permute-start | bytes 82952 | tf_op jit(solution)/shard_map/ppermute | solution.py:152
  351.5 6.3 %collective-permute-start.12 = (f32[4608]{0:T(1024)S(1)}, f32[4608]{0:T(1024)S(1)}, u32[]{:S(2)}, u32[]{:S(2)}) collective-permute-start(f32[4608]{0:T(1024)S(1)} %slice.129), channel_id=1, source_target_pairs={{0,1},{1,0},{2,3},{3,2},{4,5},{5,4},{6,7},{7,6},{8,9},{9,8},{10,11... | collective-permute-start | bytes 55304 | tf_op jit(solution)/shard_map/ppermute | solution.py:152
  356.0 43.5 %collective-permute-start.7 = (f32[512,768]{1,0:T(8,128)}, f32[512,768]{1,0:T(8,128)}, u32[]{:S(2)}, u32[]{:S(2)}) collective-permute-start(f32[512,768]{1,0:T(8,128)} %multiply_add_fusion.2), channel_id=1, source_target_pairs={{0,1},{1,0},{2,3},{3,2},{4,5},{5,4},{6,7},{7,6},{8,9},{9,8},{10,11... | collective-permute-start | bytes 4718600 | tf_op jit(solution)/shard_map/ppermute | solution.py:104
  360.6 19.6 %collective-permute-start.14 = (f32[2,2,48,3,384]{4,2,3,1,0:T(8,128)S(1)}, f32[2,2,48,3,384]{4,2,3,1,0:T(8,128)S(1)}, u32[]{:S(2)}, u32[]{:S(2)}) collective-permute-start(f32[2,2,48,3,384]{4,2,3,1,0:T(8,128)S(1)} %dynamic-slice_bitcast_fusion.2), channel_id=1, source_target_pairs={{0,4},{2,6},{4,0},{6,2},{8,12},{10,14},{12,8},{14,10},{16,20},{18,... | collective-permute-start | bytes 2654216 | tf_op jit(solution)/shard_map/ppermute | solution.py:143
  362.7 20.0 %collective-permute-start.24 = (f32[48,1536]{1,0:T(8,128)S(1)}, f32[48,1536]{1,0:T(8,128)S(1)}, u32[]{:S(2)}, u32[]{:S(2)}) collective-permute-start(f32[48,1536]{1,0:T(8,128)S(1)} %dynamic-slice_bitcast_fusion.8), channel_id=1, source_target_pairs={{0,16},{2,18},{4,20},{6,22},{8,24},{10,26},{12,28},{14,30},{16,0},... | collective-permute-start | bytes 884744 | tf_op jit(solution)/shard_map/ppermute | solution.py:143
  366.2 32.5 %collective-permute-start.28 = (f32[48,1536]{1,0:T(8,128)S(1)}, f32[48,1536]{1,0:T(8,128)S(1)}, u32[]{:S(2)}, u32[]{:S(2)}) collective-permute-start(f32[48,1536]{1,0:T(8,128)S(1)} %dynamic-slice_bitcast_fusion.7), channel_id=1, source_target_pairs={{0,16},{2,18},{4,20},{6,22},{8,24},{10,26},{12,28},{14,30},{16,0},... | collective-permute-start | bytes 884744 | tf_op jit(solution)/shard_map/ppermute | solution.py:143
  380.4 18.0 %collective-permute-start.15 = (f32[2,48,3,384]{3,1,2,0:T(8,128)S(1)}, f32[2,48,3,384]{3,1,2,0:T(8,128)S(1)}, u32[]{:S(2)}, u32[]{:S(2)}) collective-permute-start(f32[2,48,3,384]{3,1,2,0:T(8,128)S(1)} %dynamic-slice_bitcast_fusion.6), channel_id=1, source_target_pairs={{0,8},{2,10},{4,12},{6,14},{8,0},{10,2},{12,4},{14,6},{16,24},{18,... | collective-permute-start | bytes 1327112 | tf_op jit(solution)/shard_map/ppermute | solution.py:143
  398.4 12.6 %collective-permute-start.16 = (f32[48,3,384]{2,0,1:T(8,128)S(1)}, f32[48,3,384]{2,0,1:T(8,128)S(1)}, u32[]{:S(2)}, u32[]{:S(2)}) collective-permute-start(f32[48,3,384]{2,0,1:T(8,128)S(1)} %dynamic-slice_bitcast_fusion.10), channel_id=1, source_target_pairs={{0,16},{2,18},{4,20},{6,22},{8,24},{10,26},{12,28},{14,30},{16,0},... | collective-permute-start | bytes 663560 | tf_op jit(solution)/shard_map/ppermute | solution.py:143
  (94 other events, 885.8 us)

commit v2 on v1

--- a/solution.py
+++ b/solution.py
@@ -4,6 +4,7 @@
 import jax.numpy as jnp
 from jax import lax
 from jax.sharding import PartitionSpec as P
+
 
 HD = 64
 
@@ -154,7 +155,7 @@
 
 
 def make_shards(ndp, nmp):
-    def shards(
+    def shards_body(
         tokens,
         doc_ids,
         ln1_gain,
@@ -172,6 +173,7 @@
         cotangent,
     ):
         m = lax.axis_index("mp")
+        w_out_other = swap_mp(w_out)
         row_count = tokens.shape[0]
         local_width = w_qkv.shape[2]
         seq_count, seq_len = doc_ids.shape
@@ -195,7 +197,7 @@
             log_totals.append(lse_s)
         mixed = jnp.stack(attended).reshape(row_count, local_width).astype(jnp.bfloat16)
         mixed_all = join_pair(mixed, swap_mp(mixed), m, 1)
-        w_out_all = join_pair(w_out, swap_mp(w_out), m, 0)
+        w_out_all = join_pair(w_out, w_out_other, m, 0)
         attn_all = jnp.dot(mixed_all, w_out_all, preferred_element_type=jnp.float32)
         after_attn = token_rows + attn_all + b_out.astype(jnp.float32)
         gain_two = ln2_gain.astype(jnp.float32)
@@ -207,10 +209,6 @@
         activated, gelu_pull = jax.vjp(gelu_tanh, up_rows)
         act_rows = activated.astype(jnp.bfloat16)
         ffn_part = jnp.dot(act_rows, w_down, preferred_element_type=jnp.float32)
-        ffn_own = scatter_rows_mp(ffn_part, m, jnp.bfloat16)
-        after_own, _ = row_halves(after_attn, m)
-        out_own = (after_own + (ffn_own + b_down.astype(jnp.float32))).astype(jnp.bfloat16)
-        block_out = gather_rows_mp(out_own, m)
 
         cot_rows = cotangent.astype(jnp.float32)
         cot_own, _ = row_halves(cot_rows, m)
@@ -228,6 +226,11 @@
         grad_after_own = cot_own + norm_back(grad_two_own, normal_two_own, inv_two_own, gain_two)
         grad_attn_own = grad_after_own.astype(jnp.bfloat16)
         grad_attn_here = gather_rows_mp(grad_attn_own, m)
+        ffn_late, grad_attn_here = lax.optimization_barrier((ffn_part, grad_attn_here))
+        ffn_own = scatter_rows_mp(ffn_late, m, jnp.bfloat16)
+        after_own, _ = row_halves(after_attn, m)
+        out_own = (after_own + (ffn_own + b_down.astype(jnp.float32))).astype(jnp.bfloat16)
+        block_out = gather_rows_mp(out_own, m)
         grad_w_out_t = jnp.einsum(
             "td,te->de", grad_attn_here, mixed, preferred_element_type=jnp.float32
         )
@@ -304,7 +307,7 @@
             vector_sum[5],
         )
 
-    return shards
+    return shards_body
 
 
 def solution(mesh):

time: 416 us -> 417 us (level)
  waiting for transfers between devices: 146 us -> 155 us
  local copies, waits for them, and re-layouts: 51.9 us -> 44.4 us
    ppermute x5, waiting for transfers between devices: 17.6 us -> 47 us  [reduce_tree(): x = x + lax.ppermute(x, name, [(i, i ^ 1 << bit) for i in range(size)])]
    ppermute x8, waiting for transfers between devices: 75.9 us -> 51.5 us  [swap_mp(): return lax.ppermute(x, 'mp', [(0, 1), (1, 0)])]
    dot_general x12, matrix products: 45.4 us -> 40.6 us  [the longest x1 9.47 us: shards_body(): jnp.einsum('td,fd->tf', cotangent, w_down, preferred_element_type=jnp.flo...]
    unnamed x176 -> x152, local copies, waits for them, and re-layouts: 12.9 us -> 9.25 us
    select_n x2 -> x3, other arithmetic: 6.8 us -> 9.16 us  [join_pair(): jnp.where(m == 0, jnp.concatenate([own, other], axis=axis), jnp.concatena...]
  transfers between devices with their start and end apart: 29 -> 29, of which waited for: 13 -> 13; matrix products, arithmetic and copies ran while one was open for 38% -> 37% of each run, Pallas kernels for 0% -> 0%
where the time goes in v2:
time: 417 us; the launch traced here: 413 us
  waiting for transfers between devices  155 us (37%)
  matrix products  101 us (24%)
  other arithmetic  79.4 us (19%)
  local copies, waits for them, and re-layouts  44.4 us (11%)
  starting transfers between devices  31.1 us (7%)
    ppermute x16, waiting for transfers between devices, scatter_dp(): got = lax.ppermute(send, 'dp', [(i, i ^ 1 << bit) for i in range(ndp)])  56.2 us
    ppermute x8, waiting for transfers between devices, swap_mp(): return lax.ppermute(x, 'mp', [(0, 1), (1, 0)])  51.5 us
    ppermute x5, waiting for transfers between devices, reduce_tree(): x = x + lax.ppermute(x, name, [(i, i ^ 1 << bit) for i in range(size)])  47 us
    dot_general x2, matrix products, attend_backward(): jnp.einsum('qhd,khd->hqk', grad_block, value_rows, preferred_element_type...  20.5 us
    convert_element_type x1, other arithmetic, attend_backward(): grad_scores = (probabilities * (grad_probs - row_dots)).astype(jnp.bfloat16)  17.9 us
    ppermute x16, starting transfers between devices, scatter_dp(): got = lax.ppermute(send, 'dp', [(i, i ^ 1 << bit) for i in range(ndp)])  15.7 us
    add x14, other arithmetic, scatter_dp(): cur = keep + got  15.4 us
    dot_general x2, matrix products, attend_backward(): jnp.einsum('hqk,qhd->khd', probabilities.astype(jnp.bfloat16), grad_block...  12.7 us
  transfers between devices with their start and end apart: 29, of which 13 were waited for; matrix products, arithmetic and copies ran while one was open for 37% of the time, Pallas kernels for 0%

profile of v2, /device:TPU:0, one launch (start us, length us, event | category | flops | bytes accessed | tf_op | source)
XLA Modules:
  0.0 413.0 jit_solution(17312718310307946835)
XLA Ops:
  6.5 3.9 fusion.42
  18.9 3.6 exponential_reduce_fusion.1
  25.0 3.6 exponential_reduce_fusion
  29.9 3.5 convolution_convert_fusion.2
  33.5 8.0 %convolution_convert_fusion.1 = bf16[6,64,512]{2,1,0:T(8,128)(2,1)S(1)} fusion(bf16[1024,6,64]{0,2,1:T(8,128)(2,1)S(1)} %add_convert_fusion.4, f32[6,512,1024]{2,1,0:T(8,128)} %copy-done.3, f32[6,512]{1,0:T(8,128)S(1)} %log_add_fusion, pred[512,1024]{1,0:T(8,128)(4,1)S(1)} %get-tuple-element.56), kind=kOutput, calls=%fused_computation.89 | convolution fusion | flops 415432704 | bytes 14299136 | tf_op jit(solution)/shard_map/hqk,khd->qhd/dot_general | solution.py:63
  57.5 21.5 %collective-permute-done.1 = bf16[384,768]{1,0:T(8,128)(2,1)} collective-permute-done((bf16[384,768]{1,0:T(8,128)(2,1)}, bf16[384,768]{1,0:T(8,128)(2,1)}, u32[]{:S(2)}, u32[]{:S(2)}) %collective-permute-start.1) | collective-permute-done | bytes 589856 | tf_op jit(solution)/shard_map/ppermute | solution.py:105
  79.0 4.9 %fusion.60 = (f32[1024]{0:T(1024)S(1)}, f32[1024,768]{1,0:T(8,128)S(1)}) fusion(f32[768]{0:T(1024)} %convert_element_type.163, bf16[384,768]{1,0:T(8,128)(2,1)} %collective-permute-done.1, bf16[384,768]{1,0:T(8,128)(2,1)} %param.21, pred[]{:T(512)S(6)} %eq.24, bf16[1024,384]{1,0:T(8,128)(2,1)} %collective-permute-done, bf16[1024,384]{1,0:T(8,128)(2,1)} %copy.59, ...), kind=kOutput, calls=%fused_computation.168 | convolution fusion | flops 1223490560 | bytes 7478273 | tf_op jit(solution)/shard_map/dot_general | solution.py:201
  89.3 9.5 %convert_reduce_fusion = (f32[1536]{0:T(1024)}, bf16[1024,1536]{1,0:T(8,128)(2,1)S(1)}, bf16[1024,1536]{1,0:T(8,128)(2,1)S(1)}) fusion(f32[1024,1536]{1,0:T(8,128)S(1)} %fusion.38, f32[1536]{0:T(1024)S(1)} %copy-done.59, bf16[1024,768]{1,0:T(8,128)(2,1)S(1)} %copy-done.42, bf16[1536,768]{1,0:T(8,128)(2,1)S(1)} %copy-done), kind=kOutput, calls=%fused_computation.24 | convolution fusion | flops 2461530624 | bytes 16527360 | tf_op jit(solution)/shard_map/td,fd->tf/dot_general | solution.py:218
  111.1 26.1 %collective-permute-done.2 = f32[512,768]{1,0:T(8,128)S(1)} collective-permute-done((f32[512,768]{1,0:T(8,128)S(1)}, f32[512,768]{1,0:T(8,128)S(1)}, u32[]{:S(2)}, u32[]{:S(2)}) %collective-permute-start.2) | collective-permute-done | bytes 1572896 | tf_op jit(solution)/shard_map/ppermute | solution.py:105
  153.5 3.9 collective-permute-done.3
  161.5 4.7 %fusion.50 = f32[6,64,1024]{2,1,0:T(8,128)} fusion(bf16[512,6,64]{0,2,1:T(8,128)(2,1)S(1)} %bitcast.189, f32[6,512,1024]{2,1,0:T(8,128)S(1)} %bitcast.163, f32[6,512]{1,0:T(8,128)S(1)} %copy-done.46, pred[512,1024]{1,0:T(8,128)(4,1)S(1)} %copy-done.11), kind=kOutput, calls=%fused_computation.163 | convolution fusion | flops 415236096 | bytes 15085568 | tf_op jit(solution)/shard_map/hqk,qhd->khd/dot_general | solution.py:95
  168.9 8.1 %convert_reduce_fusion.3 = (f32[6,64]{1,0:T(8,128)S(1)}, bf16[6,64,1024]{2,1,0:T(8,128)(2,1)}) fusion(f32[6,64,1024]{2,1,0:T(8,128)} %fusion.50, bf16[512,6,64]{0,2,1:T(8,128)(2,1)S(1)} %bitcast.191, f32[6,512,1024]{2,1,0:T(8,128)} %copy-done.3, f32[6,512]{1,0:T(8,128)S(1)} %copy-done.48, pred[512,1024]{1,0:T(8,128)(4,1)S(1)} %copy-done.13), kind=kOutput, calls=%fused_computation.66 | convolution fusion | flops 416808576 | bytes 15873536 | tf_op jit(solution)/shard_map/hqk,qhd->khd/dot_general | solution.py:95
  183.4 10.5 %multiply_reduce_fusion = (f32[6,512]{1,0:T(8,128)S(1)}, f32[6,512,1024]{2,1,0:T(8,128)}) fusion(f32[6,512,1024]{2,1,0:T(8,128)} %copy-done.3, f32[6,512]{1,0:T(8,128)S(1)} %copy-done.48, pred[512,1024]{1,0:T(8,128)(4,1)S(1)} %copy-done.13, bf16[512,6,64]{0,2,1:T(8,128)(2,1)} %bitcast.192, bf16[1024,6,64]{0,2,1:T(8,128)(2,1)S(1)} %copy-done.22), kind=kOutput, calls=%fused_computation.1 | convolution fusion | flops 418378752 | bytes 26894336 | tf_op jit(solution)/shard_map/qhd,khd->hqk/dot_general | solution.py:83
  193.8 10.1 %multiply_reduce_fusion.1 = (f32[6,512]{1,0:T(8,128)S(1)}, f32[6,512,1024]{2,1,0:T(8,128)}) fusion(f32[6,512,1024]{2,1,0:T(8,128)} %copy-done.2, f32[6,512]{1,0:T(8,128)S(1)} %copy-done.46, pred[512,1024]{1,0:T(8,128)(4,1)S(1)} %copy-done.11, bf16[512,6,64]{0,2,1:T(8,128)(2,1)S(1)} %bitcast.190, bf16[1024,6,64]{0,2,1:T(8,128)(2,1)S(1)} %copy-done.22), kind=kOutput, calls=%fused_computation.3 | convolution fusion | flops 418378752 | bytes 26894336 | tf_op jit(solution)/shard_map/qhd,khd->hqk/dot_general | solution.py:83
  210.0 17.9 %multiply_convert_fusion = (bf16[6,512,1024]{2,1,0:T(8,128)(2,1)}, bf16[6,512,1024]{2,1,0:T(8,128)(2,1)}) fusion(f32[6,512,1024]{2,1,0:T(8,128)} %get-tuple-element.68, f32[6,512,1024]{2,1,0:T(8,128)} %copy-done.3, f32[6,512]{1,0:T(8,128)S(1)} %get-tuple-element.67, f32[6,512]{1,0:T(8,128)S(1)} %copy-done.48, pred[512,1024]{1,0:T(8,128)(4,1)S(1)} %copy-done.13, ...), kind=kLoop, calls=%fused_computation | loop fusion | flops 37748736 | bytes 64012288 | tf_op jit(solution)/shard_map/convert_element_type | solution.py:87
  227.9 4.1 %fusion.63 = f32[6,64,1024]{2,1,0:T(8,128)S(1)} fusion(bf16[512,6,64]{0,2,1:T(8,128)(2,1)S(1)} %bitcast.179, bf16[6,512,1024]{2,1,0:T(8,128)(2,1)} %get-tuple-element.72), kind=kOutput, calls=%fused_computation.171 | convolution fusion | flops 402653184 | bytes 8257536 | tf_op jit(solution)/shard_map/hqk,qhd->khd/dot_general | solution.py:92
  245.7 3.7 convolution_bitcast_fusion
  256.1 17.2 %collective-permute-done.18 = f32[2,2,48,384]{3,2,1,0:T(8,128)S(1)} collective-permute-done((f32[2,2,48,384]{3,2,1,0:T(8,128)S(1)}, f32[2,2,48,384]{3,2,1,0:T(8,128)S(1)}, u32[]{:S(2)}, u32[]{:S(2)}) %collective-permute-start.18) | collective-permute-done | bytes 294944 | tf_op jit(solution)/shard_map/ppermute | solution.py:144
  301.9 14.7 %collective-permute-done.10 = f32[6912]{0:T(1024)S(1)} collective-permute-done((f32[6912]{0:T(1024)S(1)}, f32[6912]{0:T(1024)S(1)}, u32[]{:S(2)}, u32[]{:S(2)}) %collective-permute-start.10) | collective-permute-done | bytes 27680 | tf_op jit(solution)/shard_map/ppermute | solution.py:153
  329.6 29.3 %collective-permute-done.12 = f32[4608]{0:T(1024)S(1)} collective-permute-done((f32[4608]{0:T(1024)S(1)}, f32[4608]{0:T(1024)S(1)}, u32[]{:S(2)}, u32[]{:S(2)}) %collective-permute-start.12) | collective-permute-done | bytes 18464 | tf_op jit(solution)/shard_map/ppermute | solution.py:153
  367.8 13.9 %collective-permute-done.14 = f32[2,2,48,3,384]{4,2,3,1,0:T(8,128)S(1)} collective-permute-done((f32[2,2,48,3,384]{4,2,3,1,0:T(8,128)S(1)}, f32[2,2,48,3,384]{4,2,3,1,0:T(8,128)S(1)}, u32[]{:S(2)}, u32[]{:S(2)}) %collective-permute-start.14) | collective-permute-done | bytes 884768 | tf_op jit(solution)/shard_map/ppermute | solution.py:144
  385.6 14.3 %collective-permute-done.15 = f32[2,48,3,384]{3,1,2,0:T(8,128)S(1)} collective-permute-done((f32[2,48,3,384]{3,1,2,0:T(8,128)S(1)}, f32[2,48,3,384]{3,1,2,0:T(8,128)S(1)}, u32[]{:S(2)}, u32[]{:S(2)}) %collective-permute-start.15) | collective-permute-done | bytes 442400 | tf_op jit(solution)/shard_map/ppermute | solution.py:144
  400.8 5.1 %maximum_select_fusion = f32[1024,768]{1,0:T(8,128)} fusion(f32[512,768]{1,0:T(8,128)} %collective-permute-done.7, f32[512,768]{1,0:T(8,128)} %multiply_add_fusion.2, pred[]{:T(512)S(6)} %eq.24), kind=kLoop, calls=%fused_computation.33 | loop fusion | flops 2359296 | bytes 6291457 | tf_op jit(solution)/shard_map/jit(_where)/select_n | solution.py:116
  405.9 6.1 %collective-permute-done.16 = f32[48,3,384]{2,0,1:T(8,128)S(1)} collective-permute-done((f32[48,3,384]{2,0,1:T(8,128)S(1)}, f32[48,3,384]{2,0,1:T(8,128)S(1)}, u32[]{:S(2)}, u32[]{:S(2)}) %collective-permute-start.16) | collective-permute-done | bytes 221216 | tf_op jit(solution)/shard_map/ppermute | solution.py:144
  (330 shorter events, 162.8 us)
Async XLA Ops:
  45.5 33.5 %collective-permute-start = (bf16[1024,384]{1,0:T(8,128)(2,1)}, bf16[1024,384]{1,0:T(8,128)(2,1)}, u32[]{:S(2)}, u32[]{:S(2)}) collective-permute-start(bf16[1024,384]{1,0:T(8,128)(2,1)} %copy.59), channel_id=1, source_target_pairs={{0,1},{1,0},{2,3},{3,2},{4,5},{5,4},{6,7},{7,6},{8,9},{9,8},{10,11... | collective-permute-start | bytes 2359304 | tf_op jit(solution)/shard_map/ppermute | solution.py:105
  48.5 30.5 %collective-permute-start.1 = (bf16[384,768]{1,0:T(8,128)(2,1)}, bf16[384,768]{1,0:T(8,128)(2,1)}, u32[]{:S(2)}, u32[]{:S(2)}) collective-permute-start(bf16[384,768]{1,0:T(8,128)(2,1)} %param.21), channel_id=1, source_target_pairs={{0,1},{1,0},{2,3},{3,2},{4,5},{5,4},{6,7},{7,6},{8,9},{9,8},{10,11... | collective-permute-start | bytes 1769480 | tf_op jit(solution)/shard_map/ppermute | solution.py:105
  101.6 35.6 %collective-permute-start.2 = (f32[512,768]{1,0:T(8,128)S(1)}, f32[512,768]{1,0:T(8,128)S(1)}, u32[]{:S(2)}, u32[]{:S(2)}) collective-permute-start(f32[512,768]{1,0:T(8,128)S(1)} %constant_dynamic-slice_fusion.7), channel_id=1, source_target_pairs={{0,1},{1,0},{2,3},{3,2},{4,5},{5,4},{6,7},{7,6},{8,9},{9,8},{10,11... | collective-permute-start | bytes 4718600 | tf_op jit(solution)/shard_map/ppermute | solution.py:105
  139.6 17.8 %collective-permute-start.3 = (bf16[512,768]{1,0:T(8,128)(2,1)S(1)}, bf16[512,768]{1,0:T(8,128)(2,1)S(1)}, u32[]{:S(2)}, u32[]{:S(2)}) collective-permute-start(bf16[512,768]{1,0:T(8,128)(2,1)S(1)} %get-tuple-element.29), channel_id=1, source_target_pairs={{0,1},{1,0},{2,3},{3,2},{4,5},{5,4},{6,7},{7,6},{8,9},{9,8},{10,11... | collective-permute-start | bytes 2359304 | tf_op jit(solution)/shard_map/ppermute | solution.py:105
  147.4 56.5 %collective-permute-start.21 = (f32[2,2,2,48,1536]{4,3,1,0,2:T(8,128)}, f32[2,2,2,48,1536]{4,3,1,0,2:T(8,128)}, u32[]{:S(2)}, u32[]{:S(2)}) collective-permute-start(f32[2,2,2,48,1536]{4,3,1,0,2:T(8,128)} %bitcast.160), channel_id=1, source_target_pairs={{0,2},{2,0},{4,6},{6,4},{8,10},{10,8},{12,14},{14,12},{16,18},{18,... | collective-permute-start | bytes 7077896 | tf_op jit(solution)/shard_map/ppermute | solution.py:144
  147.4 87.9 %collective-permute-start.25 = (f32[2,2,2,48,1536]{4,3,1,0,2:T(8,128)}, f32[2,2,2,48,1536]{4,3,1,0,2:T(8,128)}, u32[]{:S(2)}, u32[]{:S(2)}) collective-permute-start(f32[2,2,2,48,1536]{4,3,1,0,2:T(8,128)} %bitcast.159), channel_id=1, source_target_pairs={{0,2},{2,0},{4,6},{6,4},{8,10},{10,8},{12,14},{14,12},{16,18},{18,... | collective-permute-start | bytes 7077896 | tf_op jit(solution)/shard_map/ppermute | solution.py:144
  160.2 118.5 %collective-permute-start.4 = (bf16[512,768]{1,0:T(8,128)(2,1)}, bf16[512,768]{1,0:T(8,128)(2,1)}, u32[]{:S(2)}, u32[]{:S(2)}) collective-permute-start(bf16[512,768]{1,0:T(8,128)(2,1)} %dynamic-slice_convert_fusion), channel_id=1, source_target_pairs={{0,1},{1,0},{2,3},{3,2},{4,5},{5,4},{6,7},{7,6},{8,9},{9,8},{10,11... | collective-permute-start | bytes 2359304 | tf_op jit(solution)/shard_map/ppermute | solution.py:105
  183.3 67.2 %collective-permute-start.17 = (f32[2,2,2,48,384]{4,3,2,1,0:T(8,128)}, f32[2,2,2,48,384]{4,3,2,1,0:T(8,128)}, u32[]{:S(2)}, u32[]{:S(2)}) collective-permute-start(f32[2,2,2,48,384]{4,3,2,1,0:T(8,128)} %dynamic-slice_bitcast_fusion.5), channel_id=1, source_target_pairs={{0,2},{2,0},{4,6},{6,4},{8,10},{10,8},{12,14},{14,12},{16,18},{18,... | collective-permute-start | bytes 1769480 | tf_op jit(solution)/shard_map/ppermute | solution.py:144
  208.5 78.6 %collective-permute-start.22 = (f32[2,2,48,1536]{3,2,1,0:T(8,128)}, f32[2,2,48,1536]{3,2,1,0:T(8,128)}, u32[]{:S(2)}, u32[]{:S(2)}) collective-permute-start(f32[2,2,48,1536]{3,2,1,0:T(8,128)} %dynamic-slice_bitcast_fusion.1), channel_id=1, source_target_pairs={{0,4},{2,6},{4,0},{6,2},{8,12},{10,14},{12,8},{14,10},{16,20},{18,... | collective-permute-start | bytes 3538952 | tf_op jit(solution)/shard_map/ppermute | solution.py:144
  238.7 50.8 %collective-permute-start.26 = (f32[2,2,48,1536]{3,2,1,0:T(8,128)}, f32[2,2,48,1536]{3,2,1,0:T(8,128)}, u32[]{:S(2)}, u32[]{:S(2)}) collective-permute-start(f32[2,2,48,1536]{3,2,1,0:T(8,128)} %dynamic-slice_bitcast_fusion), channel_id=1, source_target_pairs={{0,4},{2,6},{4,0},{6,2},{8,12},{10,14},{12,8},{14,10},{16,20},{18,... | collective-permute-start | bytes 3538952 | tf_op jit(solution)/shard_map/ppermute | solution.py:144
  249.6 42.4 %collective-permute-start.6 = (f32[512,768]{1,0:T(8,128)S(1)}, f32[512,768]{1,0:T(8,128)S(1)}, u32[]{:S(2)}, u32[]{:S(2)}) collective-permute-start(f32[512,768]{1,0:T(8,128)S(1)} %constant_dynamic-slice_fusion.6), channel_id=1, source_target_pairs={{0,1},{1,0},{2,3},{3,2},{4,5},{5,4},{6,7},{7,6},{8,9},{9,8},{10,11... | collective-permute-start | bytes 4718600 | tf_op jit(solution)/shard_map/ppermute | solution.py:105
  252.0 21.4 %collective-permute-start.18 = (f32[2,2,48,384]{3,2,1,0:T(8,128)S(1)}, f32[2,2,48,384]{3,2,1,0:T(8,128)S(1)}, u32[]{:S(2)}, u32[]{:S(2)}) collective-permute-start(f32[2,2,48,384]{3,2,1,0:T(8,128)S(1)} %dynamic-slice_bitcast_fusion.9), channel_id=1, source_target_pairs={{0,4},{2,6},{4,0},{6,2},{8,12},{10,14},{12,8},{14,10},{16,20},{18,... | collective-permute-start | bytes 884744 | tf_op jit(solution)/shard_map/ppermute | solution.py:144
  278.6 80.9 %collective-permute-start.13 = (f32[2,2,2,48,3,384]{5,3,4,2,1,0:T(8,128)}, f32[2,2,2,48,3,384]{5,3,4,2,1,0:T(8,128)}, u32[]{:S(2)}, u32[]{:S(2)}) collective-permute-start(f32[2,2,2,48,3,384]{5,3,4,2,1,0:T(8,128)} %bitcast.161), channel_id=1, source_target_pairs={{0,2},{2,0},{4,6},{6,4},{8,10},{10,8},{12,14},{14,12},{16,18},{18,... | collective-permute-start | bytes 5308424 | tf_op jit(solution)/shard_map/ppermute | solution.py:144
  285.9 38.5 %collective-permute-start.5 = (bf16[512,768]{1,0:T(8,128)(2,1)}, bf16[512,768]{1,0:T(8,128)(2,1)}, u32[]{:S(2)}, u32[]{:S(2)}) collective-permute-start(bf16[512,768]{1,0:T(8,128)(2,1)} %add_convert_fusion.3), channel_id=1, source_target_pairs={{0,1},{1,0},{2,3},{3,2},{4,5},{5,4},{6,7},{7,6},{8,9},{9,8},{10,11... | collective-permute-start | bytes 2359304 | tf_op jit(solution)/shard_map/ppermute | solution.py:105
  288.5 73.8 %collective-permute-start.23 = (f32[2,48,1536]{2,1,0:T(8,128)S(1)}, f32[2,48,1536]{2,1,0:T(8,128)}, u32[]{:S(2)}, u32[]{:S(2)}) collective-permute-start(f32[2,48,1536]{2,1,0:T(8,128)S(1)} %dynamic-slice_bitcast_fusion.4), channel_id=1, source_target_pairs={{0,8},{2,10},{4,12},{6,14},{8,0},{10,2},{12,4},{14,6},{16,24},{18,... | collective-permute-start | bytes 1769480 | tf_op jit(solution)/shard_map/ppermute | solution.py:144
  295.9 68.2 %collective-permute-start.27 = (f32[2,48,1536]{2,1,0:T(8,128)}, f32[2,48,1536]{2,1,0:T(8,128)}, u32[]{:S(2)}, u32[]{:S(2)}) collective-permute-start(f32[2,48,1536]{2,1,0:T(8,128)} %dynamic-slice_bitcast_fusion.3), channel_id=1, source_target_pairs={{0,8},{2,10},{4,12},{6,14},{8,0},{10,2},{12,4},{14,6},{16,24},{18,... | collective-permute-start | bytes 1769480 | tf_op jit(solution)/shard_map/ppermute | solution.py:144
  301.3 15.4 %collective-permute-start.10 = (f32[6912]{0:T(1024)S(1)}, f32[6912]{0:T(1024)S(1)}, u32[]{:S(2)}, u32[]{:S(2)}) collective-permute-start(f32[6912]{0:T(1024)S(1)} %add.326), channel_id=1, source_target_pairs={{0,8},{2,10},{4,12},{6,14},{8,0},{10,2},{12,4},{14,6},{16,24},{18,... | collective-permute-start | bytes 82952 | tf_op jit(solution)/shard_map/ppermute | solution.py:153
  322.9 77.9 %collective-permute-start.7 = (f32[512,768]{1,0:T(8,128)}, f32[512,768]{1,0:T(8,128)}, u32[]{:S(2)}, u32[]{:S(2)}) collective-permute-start(f32[512,768]{1,0:T(8,128)} %multiply_add_fusion.2), channel_id=1, source_target_pairs={{0,1},{1,0},{2,3},{3,2},{4,5},{5,4},{6,7},{7,6},{8,9},{9,8},{10,11... | collective-permute-start | bytes 4718600 | tf_op jit(solution)/shard_map/ppermute | solution.py:105
  324.4 34.4 %collective-permute-start.12 = (f32[4608]{0:T(1024)S(1)}, f32[4608]{0:T(1024)S(1)}, u32[]{:S(2)}, u32[]{:S(2)}) collective-permute-start(f32[4608]{0:T(1024)S(1)} %slice.129), channel_id=1, source_target_pairs={{0,1},{1,0},{2,3},{3,2},{4,5},{5,4},{6,7},{7,6},{8,9},{9,8},{10,11... | collective-permute-start | bytes 55304 | tf_op jit(solution)/shard_map/ppermute | solution.py:153
  361.8 19.9 %collective-permute-start.14 = (f32[2,2,48,3,384]{4,2,3,1,0:T(8,128)S(1)}, f32[2,2,48,3,384]{4,2,3,1,0:T(8,128)S(1)}, u32[]{:S(2)}, u32[]{:S(2)}) collective-permute-start(f32[2,2,48,3,384]{4,2,3,1,0:T(8,128)S(1)} %dynamic-slice_bitcast_fusion.2), channel_id=1, source_target_pairs={{0,4},{2,6},{4,0},{6,2},{8,12},{10,14},{12,8},{14,10},{16,20},{18,... | collective-permute-start | bytes 2654216 | tf_op jit(solution)/shard_map/ppermute | solution.py:144
  363.5 21.3 %collective-permute-start.24 = (f32[48,1536]{1,0:T(8,128)S(1)}, f32[48,1536]{1,0:T(8,128)S(1)}, u32[]{:S(2)}, u32[]{:S(2)}) collective-permute-start(f32[48,1536]{1,0:T(8,128)S(1)} %dynamic-slice_bitcast_fusion.8), channel_id=1, source_target_pairs={{0,16},{2,18},{4,20},{6,22},{8,24},{10,26},{12,28},{14,30},{16,0},... | collective-permute-start | bytes 884744 | tf_op jit(solution)/shard_map/ppermute | solution.py:144
  365.3 34.7 %collective-permute-start.28 = (f32[48,1536]{1,0:T(8,128)S(1)}, f32[48,1536]{1,0:T(8,128)S(1)}, u32[]{:S(2)}, u32[]{:S(2)}) collective-permute-start(f32[48,1536]{1,0:T(8,128)S(1)} %dynamic-slice_bitcast_fusion.7), channel_id=1, source_target_pairs={{0,16},{2,18},{4,20},{6,22},{8,24},{10,26},{12,28},{14,30},{16,0},... | collective-permute-start | bytes 884744 | tf_op jit(solution)/shard_map/ppermute | solution.py:144
  381.8 18.1 %collective-permute-start.15 = (f32[2,48,3,384]{3,1,2,0:T(8,128)S(1)}, f32[2,48,3,384]{3,1,2,0:T(8,128)S(1)}, u32[]{:S(2)}, u32[]{:S(2)}) collective-permute-start(f32[2,48,3,384]{3,1,2,0:T(8,128)S(1)} %dynamic-slice_bitcast_fusion.6), channel_id=1, source_target_pairs={{0,8},{2,10},{4,12},{6,14},{8,0},{10,2},{12,4},{14,6},{16,24},{18,... | collective-permute-start | bytes 1327112 | tf_op jit(solution)/shard_map/ppermute | solution.py:144
  399.9 12.1 %collective-permute-start.16 = (f32[48,3,384]{2,0,1:T(8,128)S(1)}, f32[48,3,384]{2,0,1:T(8,128)S(1)}, u32[]{:S(2)}, u32[]{:S(2)}) collective-permute-start(f32[48,3,384]{2,0,1:T(8,128)S(1)} %dynamic-slice_bitcast_fusion.10), channel_id=1, source_target_pairs={{0,16},{2,18},{4,20},{6,22},{8,24},{10,26},{12,28},{14,30},{16,0},... | collective-permute-start | bytes 663560 | tf_op jit(solution)/shard_map/ppermute | solution.py:144
  (82 other events, 618.5 us)
